TPU v7x, 128 devices: a whole 4x4x4 slice. The times are simulated.
128 devices in a mesh: req: 16 (over y, z_hi, core), kv: 8 (over z_lo, x).
Axes of the slice: x: 4, y: 4, z: 4 (z_hi: 2, z_lo: 2; z = z_hi * 2 + z_lo), core: 2. Of those that a mesh axis runs over, the one named last changes fastest.
Arguments:
- tokens: bfloat16 [1024, 8192], P(None, 'req'), may hold values from -40 to 40
- norm_in: bfloat16 [8192], P('req'), may hold values from 0.099609375 to 1.8984375
- w_qkv: bfloat16 [8192, 10240], P('req', 'kv'), may hold values from -0.0625 to 0.0625
- qkv_bias: bfloat16 [10240], P('kv'), may hold values from -12 to 12
- w_out: bfloat16 [8192, 8192], P('kv', 'req'), may hold values from -0.0625 to 0.0625
- norm_mid: bfloat16 [8192], P('req'), may hold values from 0.099609375 to 1.8984375
- w_gate: bfloat16 [8192, 29568], P('req', 'kv'), may hold values from -0.0625 to 0.0625
- w_up: bfloat16 [8192, 29568], P('req', 'kv'), may hold values from -0.0625 to 0.0625
- w_down: bfloat16 [29568, 8192], P('kv', 'req'), may hold values from -0.03125 to 0.03125
- short_keys: bfloat16 [1024, 256, 8, 128], P('req', None, 'kv'), may hold values from -310 to 310
- short_values: bfloat16 [1024, 256, 8, 128], P('req', None, 'kv'), may hold values from -6 to 6
- short_len: int32 [1024], P('req'), may hold values from 1 to 256, 131072 in all
- long_keys: bfloat16 [16, 8192, 8, 128], P('req', None, 'kv'), may hold values from -310 to 310
- long_values: bfloat16 [16, 8192, 8, 128], P('req', None, 'kv'), may hold values from -6 to 6
- long_len: int32 [16], replicated, may hold values from 0 to 8192, as said below
- positions: int32 [1024], P('req'), may hold values from 0 to 32767
Outputs:
- layer_out: bfloat16 [1024, 8192], P(None, 'req')
Inputs may be any that keep to these rules, and one draw needn't show every extreme that they name: `short_len`: short lengths sum to 131072 and the largest is 256. `long_len`: exactly 8 segments are live, the others have length 0; live ones hold at least 4096 slots and one holds 8192.
All inputs are finite; a program needn't handle non-finite values. No bound on the sum of `short_len` on one device may be relied on, other than what follows from the above.
Results may differ from a plain program's by a relative error of at most 0.0085.
Values may be sent and summed in bfloat16 or wider, within the bound.
No kernel may reach another device: no remote copies, remote signals or barrier semaphores. Data moves between devices by JAX's collectives and lax.ppermute only.
A program may use at most 128 MiB of HBM per device.

v0:
```python
import jax
import jax.numpy as jnp
from jax import lax
from jax.sharding import PartitionSpec as P

D = 8192
HD = 128
SHORT_CAP = 256
LONG_CAP = 8192
REQ_DEV = 64
GROUP = 8


EPS = 1e-06
THETA = 1000000.0
NEGATIVE = -1e30


def rotate(values, angles):
    half = values.shape[-1] // 2
    first = values[..., :half]
    second = values[..., half:]
    cosine = jnp.cos(angles)
    sine = jnp.sin(angles)
    return jnp.concatenate(
        [first * cosine - second * sine, second * cosine + first * sine], axis=-1
    )


def weigh(short_raw, own_raw, short_values, own_values, peak):
    short_weights = jnp.exp(short_raw - peak[..., None])
    own_weights = jnp.exp(own_raw - peak)
    total = jnp.sum(short_weights, axis=3) + own_weights
    summed = jnp.einsum(
        "rhgs,rshd->rhgd",
        short_weights.astype(jnp.bfloat16),
        short_values,
        preferred_element_type=jnp.float32,
    )
    summed = summed + jnp.einsum(
        "rhg,rhd->rhgd",
        own_weights.astype(jnp.bfloat16),
        own_values,
        preferred_element_type=jnp.float32,
    )
    return (total, summed)


def per_device(
    tokens,
    norm_in,
    w_qkv,
    qkv_bias,
    w_out,
    norm_mid,
    w_gate,
    w_up,
    w_down,
    short_keys,
    short_values,
    short_len,
    long_keys,
    long_values,
    long_len,
    positions,
):
    heads_here = short_keys.shape[2]
    scale = HD ** (-0.5)
    wide = tokens.astype(jnp.float32)
    square_in = lax.psum(jnp.sum(wide * wide, axis=1), "req")
    normed = (
        wide * lax.rsqrt(square_in / D + EPS)[:, None] * norm_in.astype(jnp.float32)[None, :]
    ).astype(jnp.bfloat16)
    block = normed
    united = lax.psum_scatter(
        jnp.dot(block, w_qkv, preferred_element_type=jnp.float32).astype(jnp.bfloat16),
        "req",
        scatter_dimension=0,
        tiled=True,
    ).astype(jnp.float32)
    united = (united + qkv_bias.astype(jnp.float32)[None, :]).reshape(
        REQ_DEV, heads_here, GROUP + 2, HD
    )
    inv_freq = THETA ** (-(2.0 * jnp.arange(HD // 2, dtype=jnp.float32)) / HD)
    angles = positions.astype(jnp.float32)[:, None] * inv_freq[None, :]
    queries = rotate(united[:, :, :GROUP], angles[:, None, None, :]).astype(jnp.bfloat16)
    new_keys = rotate(united[:, :, GROUP], angles[:, None, :]).astype(jnp.bfloat16)
    new_values = united[:, :, GROUP + 1].astype(jnp.bfloat16)
    short_raw = (
        jnp.einsum("rhgd,rshd->rhgs", queries, short_keys, preferred_element_type=jnp.float32)
        * scale
    )
    live = jnp.arange(SHORT_CAP)[None, :] < short_len[:, None]
    short_raw = jnp.where(live[:, None, None, :], short_raw, NEGATIVE)
    own_raw = (
        jnp.einsum("rhgd,rhd->rhg", queries, new_keys, preferred_element_type=jnp.float32) * scale
    )
    peak = jnp.maximum(jnp.max(short_raw, axis=3), own_raw)
    slot = lax.axis_index("req")
    slot_len = lax.dynamic_index_in_dim(long_len, slot, 0, keepdims=False)
    long_raw = (
        jnp.einsum("hgd,lhd->hgl", queries[0], long_keys[0], preferred_element_type=jnp.float32)
        * scale
    )
    long_live = jnp.arange(LONG_CAP) < slot_len
    long_raw = jnp.where(long_live[None, None, :], long_raw, NEGATIVE)
    first_peak = jnp.maximum(peak[0], jnp.max(long_raw, axis=2))
    peak = jnp.concatenate([first_peak[None], peak[1:]], axis=0)
    total, summed = weigh(short_raw, own_raw, short_values, new_values, peak)
    long_weights = jnp.where(
        long_live[None, None, :], jnp.exp(long_raw - first_peak[:, :, None]), 0.0
    )
    long_summed = jnp.einsum(
        "hgl,lhd->hgd",
        long_weights.astype(jnp.bfloat16),
        long_values[0],
        preferred_element_type=jnp.float32,
    )
    total = total.at[0].add(jnp.sum(long_weights, axis=2))
    summed = summed.at[0].add(long_summed)
    attended = (
        (summed / total[..., None]).astype(jnp.bfloat16).reshape(REQ_DEV, heads_here * GROUP * HD)
    )
    out_part = jnp.dot(
        lax.all_gather(attended, "req", axis=0, tiled=True),
        w_out,
        preferred_element_type=jnp.float32,
    )
    projected = lax.psum(out_part.astype(jnp.bfloat16), "kv").astype(jnp.float32)
    residual = lax.optimization_barrier((wide + projected).astype(jnp.bfloat16))
    resid_wide = residual.astype(jnp.float32)
    square_mid = lax.psum(jnp.sum(resid_wide * resid_wide, axis=1), "req")
    mixed_in = (
        resid_wide
        * lax.rsqrt(square_mid / D + EPS)[:, None]
        * norm_mid.astype(jnp.float32)[None, :]
    ).astype(jnp.bfloat16)
    block = mixed_in
    gate_up = lax.psum_scatter(
        jnp.concatenate(
            [
                jnp.dot(block, w_gate, preferred_element_type=jnp.float32),
                jnp.dot(block, w_up, preferred_element_type=jnp.float32),
            ],
            axis=1,
        ).astype(jnp.bfloat16),
        "req",
        scatter_dimension=0,
        tiled=True,
    ).astype(jnp.float32)
    units = w_gate.shape[1]
    act = (jax.nn.silu(gate_up[:, :units]) * gate_up[:, units:]).astype(jnp.bfloat16)
    down_part = jnp.dot(
        lax.all_gather(act, "req", axis=0, tiled=True), w_down, preferred_element_type=jnp.float32
    )
    down = lax.psum(down_part.astype(jnp.bfloat16), "kv").astype(jnp.float32)
    return (resid_wide + down).astype(jnp.bfloat16)


def solution(mesh):
    placed = (
        P(None, "req"),
        P("req"),
        P("req", "kv"),
        P("kv"),
        P("kv", "req"),
        P("req"),
        P("req", "kv"),
        P("req", "kv"),
        P("kv", "req"),
        P("req", None, "kv", None),
        P("req", None, "kv", None),
        P("req"),
        P("req", None, "kv", None),
        P("req", None, "kv", None),
        P(),
        P("req"),
    )
    return jax.shard_map(
        per_device, mesh=mesh, in_specs=placed, out_specs=P(None, "req"), check_vma=False
    )
```

profile of v0, /device:TPU:0, one launch (start us, length us, event | category | flops | bytes accessed | tf_op | source)
XLA Modules:
  0.0 643.7 jit_solution(7566164416862273333)
XLA Ops:
  6.5 0.8 convert_element_type.91
  7.4 1.5 fusion.5
  8.9 39.0 %psum.28 = f32[1024]{0:T(1024)S(1)} all-reduce(f32[1024]{0:T(1024)S(1)} %fusion.5), channel_id=1, replica_groups=mesh['req'=16,'kv'=8] {'req'}, use_global_device_ids=true, to_apply=%region_1.0 | all-reduce | flops 1024 | bytes 8192 | tf_op jit(solution)/shard_map/psum | solution.py:70
  47.9 4.7 convolution_convert_fusion.2
  54.9 68.1 %reduce-scatter.5.cloned.1.call-done = bf16[64,1280]{1,0:T(8,128)(2,1)} async-done(((bf16[1024,1280]{1,0:T(8,128)(2,1)}), bf16[64,1280]{1,0:T(8,128)(2,1)}) %reduce-scatter.5.cloned.1.call-update) | async-done | bytes 163856 | tf_op jit(solution)/shard_map/reduce_scatter | solution.py:75
  123.0 0.9 convert_add_fusion.2
  125.6 3.5 fusion.73
  130.1 3.0 fusion.22
  134.6 47.1 %all-gather.3.cloned.1.call-done = bf16[1024,1024]{1,0:T(8,128)(2,1)} async-done(((bf16[64,1024]{1,0:T(8,128)(2,1)}), bf16[1024,1024]{1,0:T(8,128)(2,1)}) %all-gather.3.cloned.1.call-update) | async-done | bytes 2097168 | tf_op jit(solution)/shard_map/all_gather | solution.py:125
  181.7 4.1 convolution_convert_fusion.4
  185.9 76.1 %all-reduce.3.cloned.1.call-done = bf16[1024,512]{1,0:T(8,128)(2,1)} async-done(((bf16[1024,512]{1,0:T(8,128)(2,1)}), bf16[1024,512]{1,0:T(8,128)(2,1)}) %all-reduce.3.cloned.1.call-update) | async-done | bytes 1048592 | tf_op jit(solution)/shard_map/psum | solution.py:129
  262.0 1.5 fusion.8
  263.7 33.3 %psum.30 = f32[1024]{0:T(1024)S(1)} all-reduce(f32[1024]{0:T(1024)S(1)} %fusion.9), channel_id=1, replica_groups=mesh['req'=16,'kv'=8] {'req'}, use_global_device_ids=true, to_apply=%region_9.10 | all-reduce | flops 1024 | bytes 8192 | tf_op jit(solution)/shard_map/psum | solution.py:132
  297.1 7.0 %convolution_convert_fusion = bf16[1024,3696]{0,1:T(8,128)(2,1)S(1)} fusion(bf16[512,3696]{0,1:T(8,128)(2,1)} %param.27, bf16[1024,512]{1,0:T(8,128)(2,1)S(1)} %fusion.8, f32[512]{0:T(512)S(1)} %convert_element_type.105, f32[1024]{0:T(1024)S(1)} %add_rsqrt_fusion), kind=kOutput, calls=%fused_computation.3 | convolution fusion | flops 3881418752 | bytes 12408832 | tf_op jit(solution)/shard_map/dot_general | solution.py:143
  304.2 4.6 convolution_convert_fusion.1
  308.7 21.5 %pad_maximum_fusion = bf16[1024,7392]{0,1:T(8,128)(2,1)} fusion(bf16[1024,3696]{0,1:T(8,128)(2,1)S(1)} %convolution_convert_fusion, bf16[1024,3696]{0,1:T(8,128)(2,1)S(1)} %convolution_convert_fusion.1), kind=kLoop, calls=%fused_computation | loop fusion | flops 30277632 | bytes 30277632 | tf_op jit(solution)/shard_map/concatenate | solution.py:140
  330.2 18.9 %copy.41 = bf16[1024,7392]{1,0:T(8,128)(2,1)} copy(bf16[1024,7392]{0,1:T(8,128)(2,1)} %pad_maximum_fusion) | data formatting | bytes 30277632
  349.2 130.7 %reduce-scatter.7.cloned.1.call-done = bf16[64,7392]{1,0:T(8,128)(2,1)} async-done(((bf16[1024,7392]{1,0:T(8,128)(2,1)}), bf16[64,7392]{1,0:T(8,128)(2,1)}) %reduce-scatter.7.cloned.1.call-update) | async-done | bytes 946192 | tf_op jit(solution)/shard_map/reduce_scatter | solution.py:139
  479.9 1.3 convert_element_type.107
  481.2 1.1 fusion.37
  482.3 67.5 %all-gather.5.cloned.1.call-done = bf16[1024,3696]{1,0:T(8,128)(2,1)} async-done(((bf16[64,3696]{1,0:T(8,128)(2,1)}), bf16[1024,3696]{1,0:T(8,128)(2,1)}) %all-gather.5.cloned.1.call-update) | async-done | bytes 7569424 | tf_op jit(solution)/shard_map/all_gather | solution.py:154
  549.8 9.4 %convolution_convert_fusion.3 = bf16[1024,512]{1,0:T(8,128)(2,1)} fusion(bf16[1024,3696]{1,0:T(8,128)(2,1)} %all-gather.5.cloned.1.call-done, bf16[3696,512]{1,0:T(8,128)(2,1)} %param.28), kind=kOutput, calls=%fused_computation.27 | convolution fusion | flops 3876061184 | bytes 12402688 | tf_op jit(solution)/shard_map/dot_general | solution.py:153
  559.3 75.1 %all-reduce.5.cloned.1.call-done = bf16[1024,512]{1,0:T(8,128)(2,1)} async-done(((bf16[1024,512]{1,0:T(8,128)(2,1)}), bf16[1024,512]{1,0:T(8,128)(2,1)}) %all-reduce.5.cloned.1.call-update) | async-done | bytes 1048592 | tf_op jit(solution)/shard_map/psum | solution.py:156
  634.3 2.5 fusion.12
  (69 shorter events, 6.6 us)
Async XLA Ops:
  6.5 118.0 %copy-start = (bf16[1,8192,1,128]{3,1,2,0:T(8,128)(2,1)S(1)}, bf16[1,8192,1,128]{3,1,2,0:T(8,128)(2,1)}, u32[]{:S(2)}) copy-start(bf16[1,8192,1,128]{3,1,2,0:T(8,128)(2,1)} %param.32) | copy-start | bytes 6291460
  6.5 116.5 %reduce-scatter.5.cloned.1.call-start = ((), (), s32[]{:S(2)}) async-start(), calls=%async_computation.2 | async-start | bytes 2785280 | tf_op jit(solution)/shard_map/reduce_scatter | solution.py:75
  52.6 0.7 copy-start.8
  52.6 0.7 copy-start.4
  52.6 0.7 copy-start.9
  52.6 2.0 copy-start.6
  52.7 129.0 %all-gather.3.cloned.1.call-start = ((), (), s32[]{:S(2)}) async-start(), calls=%async_computation.3 | async-start | bytes 2228224 | tf_op jit(solution)/shard_map/all_gather | solution.py:125
  130.1 3.1 copy-start.3
  134.5 51.3 %copy-start.5 = (bf16[512]{0:T(512)(128)(2,1)S(1)}, bf16[512]{0:T(512)(128)(2,1)}, u32[]{:S(2)}) copy-start(bf16[512]{0:T(512)(128)(2,1)} %param.25) | copy-start | bytes 3076
  134.5 127.4 %copy-start.2 = (bf16[1024,512]{1,0:T(8,128)(2,1)S(1)}, bf16[1024,512]{1,0:T(8,128)(2,1)}, u32[]{:S(2)}) copy-start(bf16[1024,512]{1,0:T(8,128)(2,1)} %param.20) | copy-start | bytes 3145732
  134.5 127.4 %all-reduce.3.cloned.1.call-start = ((), (), s32[]{:S(2)}) async-start(), calls=%async_computation.4 | async-start | bytes 2097152 | tf_op jit(solution)/shard_map/psum | solution.py:129
  185.8 294.1 %reduce-scatter.7.cloned.1.call-start = ((), (), s32[]{:S(2)}) async-start(), calls=%async_computation.7 | async-start | bytes 16154624 | tf_op jit(solution)/shard_map/reduce_scatter | solution.py:139
  297.1 7.1 %copy-start.7 = (bf16[512,3696]{0,1:T(8,128)(2,1)S(1)}, bf16[512,3696]{0,1:T(8,128)(2,1)}, u32[]{:S(2)}) copy-start(bf16[512,3696]{0,1:T(8,128)(2,1)} %param.26) | copy-start | bytes 11354116
  349.2 200.7 %all-gather.5.cloned.1.call-start = ((), (), s32[]{:S(2)}) async-start(), calls=%async_computation.5 | async-start | bytes 8077312 | tf_op jit(solution)/shard_map/all_gather | solution.py:154
  482.3 152.1 %all-reduce.5.cloned.1.call-start = ((), (), s32[]{:S(2)}) async-start(), calls=%async_computation.6 | async-start | bytes 2097152 | tf_op jit(solution)/shard_map/psum | solution.py:156
  559.2 77.6 %copy-start.1 = (bf16[1,8192,1,128]{3,1,2,0:T(8,128)(2,1)S(1)}, bf16[1,8192,1,128]{3,1,2,0:T(8,128)(2,1)}, u32[]{:S(2)}) copy-start(bf16[1,8192,1,128]{3,1,2,0:T(8,128)(2,1)} %param.32) | copy-start | bytes 6291460
Sparse Core Ops, SparseCore 0:
  52.8 70.1 reduce-scatter.4
  134.6 47.0 all-gather.2
  185.9 75.9 all-reduce.2
  349.3 130.5 reduce-scatter.6
  482.4 67.3 all-gather.4
  559.4 74.9 all-reduce.4
where the time goes:
time: 645 us; the launch traced here: 644 us
  waiting for transfers between devices  465 us (72%)
  blocking collectives  72.4 us (11%)
  matrix products  37.9 us (6%)
  other arithmetic  33.6 us (5%)
  local copies, waits for them, and re-layouts  21.2 us (3%)
  between operations  13.8 us (2%)
    reduce_scatter x1, waiting for transfers between devices, per_device(): lax.psum_scatter(jnp.concatenate([jnp.dot(block, w_gate, preferred_elemen...  131 us
    psum x1, waiting for transfers between devices, per_device(): lax.psum(out_part.astype(jnp.bfloat16), 'kv').astype(jnp.float32)  76.1 us
    psum x1, waiting for transfers between devices, per_device(): down = lax.psum(down_part.astype(jnp.bfloat16), 'kv').astype(jnp.float32)  75.1 us
    reduce_scatter x1, waiting for transfers between devices, per_device(): lax.psum_scatter(jnp.dot(block, w_qkv, preferred_element_type=jnp.float32...  68.1 us
    all_gather x1, waiting for transfers between devices, per_device(): lax.all_gather(act, 'req', axis=0, tiled=True)  67.5 us
    all_gather x1, waiting for transfers between devices, per_device(): lax.all_gather(attended, 'req', axis=0, tiled=True)  47.1 us
    psum x1, blocking collectives, per_device(): square_in = lax.psum(jnp.sum(wide * wide, axis=1), 'req')  39 us
    psum x1, blocking collectives, per_device(): square_mid = lax.psum(jnp.sum(resid_wide * resid_wide, axis=1), 'req')  33.3 us
  transfers between devices with their start and end apart: 6, of which 6 were waited for; matrix products, arithmetic and copies ran while one was open for 0% of the time, Pallas kernels for 0%

commit v1 on v0

--- a/solution.py
+++ b/solution.py
@@ -67,18 +67,17 @@
     heads_here = short_keys.shape[2]
     scale = HD ** (-0.5)
     wide = tokens.astype(jnp.float32)
+    slot = lax.axis_index("req")
     square_in = lax.psum(jnp.sum(wide * wide, axis=1), "req")
-    normed = (
-        wide * lax.rsqrt(square_in / D + EPS)[:, None] * norm_in.astype(jnp.float32)[None, :]
-    ).astype(jnp.bfloat16)
-    block = normed
+    gained = (wide * norm_in.astype(jnp.float32)[None, :]).astype(jnp.bfloat16)
     united = lax.psum_scatter(
-        jnp.dot(block, w_qkv, preferred_element_type=jnp.float32).astype(jnp.bfloat16),
+        jnp.dot(gained, w_qkv, preferred_element_type=jnp.float32).astype(jnp.bfloat16),
         "req",
         scatter_dimension=0,
         tiled=True,
     ).astype(jnp.float32)
-    united = (united + qkv_bias.astype(jnp.float32)[None, :]).reshape(
+    scale_in = lax.rsqrt(lax.dynamic_slice_in_dim(square_in, slot * REQ_DEV, REQ_DEV) / D + EPS)
+    united = (united * scale_in[:, None] + qkv_bias.astype(jnp.float32)[None, :]).reshape(
         REQ_DEV, heads_here, GROUP + 2, HD
     )
     inv_freq = THETA ** (-(2.0 * jnp.arange(HD // 2, dtype=jnp.float32)) / HD)
@@ -96,7 +95,6 @@
         jnp.einsum("rhgd,rhd->rhg", queries, new_keys, preferred_element_type=jnp.float32) * scale
     )
     peak = jnp.maximum(jnp.max(short_raw, axis=3), own_raw)
-    slot = lax.axis_index("req")
     slot_len = lax.dynamic_index_in_dim(long_len, slot, 0, keepdims=False)
     long_raw = (
         jnp.einsum("hgd,lhd->hgl", queries[0], long_keys[0], preferred_element_type=jnp.float32)
@@ -130,26 +128,26 @@
     residual = lax.optimization_barrier((wide + projected).astype(jnp.bfloat16))
     resid_wide = residual.astype(jnp.float32)
     square_mid = lax.psum(jnp.sum(resid_wide * resid_wide, axis=1), "req")
-    mixed_in = (
-        resid_wide
-        * lax.rsqrt(square_mid / D + EPS)[:, None]
-        * norm_mid.astype(jnp.float32)[None, :]
-    ).astype(jnp.bfloat16)
-    block = mixed_in
+    mixed_in = (resid_wide * norm_mid.astype(jnp.float32)[None, :]).astype(jnp.bfloat16)
+    units = w_gate.shape[1]
+    padded = -(-units // 128) * 128
+    w_gate_up = jnp.concatenate(
+        [
+            jnp.pad(w_gate, ((0, 0), (0, padded - units))),
+            jnp.pad(w_up, ((0, 0), (0, padded - units))),
+        ],
+        axis=1,
+    )
     gate_up = lax.psum_scatter(
-        jnp.concatenate(
-            [
-                jnp.dot(block, w_gate, preferred_element_type=jnp.float32),
-                jnp.dot(block, w_up, preferred_element_type=jnp.float32),
-            ],
-            axis=1,
-        ).astype(jnp.bfloat16),
+        jnp.dot(mixed_in, w_gate_up, preferred_element_type=jnp.float32).astype(jnp.bfloat16),
         "req",
         scatter_dimension=0,
         tiled=True,
     ).astype(jnp.float32)
-    units = w_gate.shape[1]
-    act = (jax.nn.silu(gate_up[:, :units]) * gate_up[:, units:]).astype(jnp.bfloat16)
+    scale_mid = lax.rsqrt(lax.dynamic_slice_in_dim(square_mid, slot * REQ_DEV, REQ_DEV) / D + EPS)
+    gate = gate_up[:, :units] * scale_mid[:, None]
+    up = gate_up[:, padded : padded + units] * scale_mid[:, None]
+    act = (jax.nn.silu(gate) * up).astype(jnp.bfloat16)
     down_part = jnp.dot(
         lax.all_gather(act, "req", axis=0, tiled=True), w_down, preferred_element_type=jnp.float32
     )

time: 645 us -> 544 us (0.84)
  waiting for transfers between devices: 465 us -> 402 us
  other arithmetic: 33.6 us -> 11.2 us
  local copies, waits for them, and re-layouts: 21.2 us -> 1.69 us
    reduce_scatter x2, waiting for transfers between devices: 199 us -> 136 us  [the longest x1 101 us: per_device(): lax.psum_scatter(jnp.dot(mixed_in, w_gate_up, preferred_element_type=jnp....]
    concatenate x1 -> x0, other arithmetic: 21.5 us -> none  [per_device(): jnp.concatenate([jnp.dot(block, w_gate, preferred_element_type=jnp.float3...]
    unnamed x23 -> x20, local copies, waits for them, and re-layouts: 20.2 us -> 0.74 us
    dot_general x3 -> x2, matrix products: 16.3 us -> 19.5 us  [the longest x1 14.7 us: per_device(): jnp.dot(mixed_in, w_gate_up, preferred_element_type=jnp.float32)]
where the time goes in v1:
time: 544 us
  waiting for transfers between devices  402 us (74%)
  blocking collectives  72.5 us (13%)
  matrix products  42.6 us (8%)
  between operations  13.8 us (3%)
  other arithmetic  11.2 us (2%)
    reduce_scatter x1, waiting for transfers between devices, per_device(): lax.psum_scatter(jnp.dot(mixed_in, w_gate_up, preferred_element_type=jnp....  101 us
    psum x1, waiting for transfers between devices, per_device(): lax.psum(out_part.astype(jnp.bfloat16), 'kv').astype(jnp.float32)  76.1 us
    psum x1, waiting for transfers between devices, per_device(): down = lax.psum(down_part.astype(jnp.bfloat16), 'kv').astype(jnp.float32)  75.1 us
    all_gather x1, waiting for transfers between devices, per_device(): lax.all_gather(act, 'req', axis=0, tiled=True)  67.5 us
    all_gather x1, waiting for transfers between devices, per_device(): lax.all_gather(attended, 'req', axis=0, tiled=True)  47.1 us
    psum x1, blocking collectives, per_device(): square_in = lax.psum(jnp.sum(wide * wide, axis=1), 'req')  39.1 us
    reduce_scatter x1, waiting for transfers between devices, per_device(): lax.psum_scatter(jnp.dot(gained, w_qkv, preferred_element_type=jnp.float3...  35 us
    psum x1, blocking collectives, per_device(): square_mid = lax.psum(jnp.sum(resid_wide * resid_wide, axis=1), 'req')  33.3 us
  transfers between devices with their start and end apart: 6, of which 6 were waited for; matrix products, arithmetic and copies ran while one was open for 0% of the time, Pallas kernels for 0%

profile of v1, /device:TPU:0, one launch (start us, length us, event | category | flops | bytes accessed | tf_op | source)
XLA Modules:
  0.0 543.8 jit_solution(6019344185695769220)
XLA Ops:
  6.5 0.8 convert_element_type.96
  7.4 4.8 convolution_convert_fusion.1
  13.2 39.1 %psum.28 = f32[1024]{0:T(1024)S(1)} all-reduce(f32[1024]{0:T(1024)S(1)} %fusion.15), channel_id=1, replica_groups=mesh['req'=16,'kv'=8] {'req'}, use_global_device_ids=true, to_apply=%region_2.0 | all-reduce | flops 1024 | bytes 8192 | tf_op jit(solution)/shard_map/psum | solution.py:71
  52.4 0.7 iota_compare_fusion.3
  53.3 35.0 %reduce-scatter.3.cloned.1.call-done = bf16[64,1280]{1,0:T(8,128)(2,1)} async-done(((bf16[1024,1280]{1,0:T(8,128)(2,1)}), bf16[64,1280]{1,0:T(8,128)(2,1)}) %reduce-scatter.3.cloned.1.call-update) | async-done | bytes 163856 | tf_op jit(solution)/shard_map/reduce_scatter | solution.py:73
  88.3 1.0 multiply_add_fusion
  89.9 0.8 fusion.84
  91.0 3.5 fusion.83
  95.5 2.9 fusion.29
  98.4 2.0 fusion.38
  100.6 0.7 copy.38
  101.4 47.1 %all-gather.3.cloned.1.call-done = bf16[1024,1024]{1,0:T(8,128)(2,1)} async-done(((bf16[64,1024]{1,0:T(8,128)(2,1)}), bf16[1024,1024]{1,0:T(8,128)(2,1)}) %all-gather.3.cloned.1.call-update) | async-done | bytes 2097168 | tf_op jit(solution)/shard_map/all_gather | solution.py:123
  148.5 4.1 convolution_convert_fusion.3
  152.6 76.1 %all-reduce.5.cloned.1.call-done = bf16[1024,512]{1,0:T(8,128)(2,1)} async-done(((bf16[1024,512]{1,0:T(8,128)(2,1)}), bf16[1024,512]{1,0:T(8,128)(2,1)}) %all-reduce.5.cloned.1.call-update) | async-done | bytes 1048592 | tf_op jit(solution)/shard_map/psum | solution.py:127
  228.8 1.5 fusion.16
  230.3 14.7 %convolution_convert_fusion = bf16[1024,7424]{1,0:T(8,128)(2,1)} fusion(bf16[512,3696]{0,1:T(8,128)(2,1)} %param.27, bf16[512,3696]{0,1:T(8,128)(2,1)} %param.26, bf16[1024,512]{1,0:T(8,128)(2,1)S(1)} %fusion.16, f32[512]{0:T(512)S(1)} %convert_element_type.110), kind=kOutput, calls=%fused_computation.4 | convolution fusion | flops 7824211968 | bytes 23824384 | tf_op jit(solution)/shard_map/dot_general | solution.py:142
  245.3 33.3 %psum.30 = f32[1024]{0:T(1024)S(1)} all-reduce(f32[1024]{0:T(1024)S(1)} %fusion.18), channel_id=1, replica_groups=mesh['req'=16,'kv'=8] {'req'}, use_global_device_ids=true, to_apply=%region_10.11 | all-reduce | flops 1024 | bytes 8192 | tf_op jit(solution)/shard_map/psum | solution.py:130
  278.7 101.1 %reduce-scatter.5.cloned.1.call-done = bf16[64,7424]{1,0:T(8,128)(2,1)} async-done(((bf16[1024,7424]{1,0:T(8,128)(2,1)}), bf16[64,7424]{1,0:T(8,128)(2,1)}) %reduce-scatter.5.cloned.1.call-update) | async-done | bytes 950288 | tf_op jit(solution)/shard_map/reduce_scatter | solution.py:141
  379.8 1.3 convert_element_type.113
  381.1 1.1 fusion.46
  382.3 67.5 %all-gather.5.cloned.1.call-done = bf16[1024,3696]{1,0:T(8,128)(2,1)} async-done(((bf16[64,3696]{1,0:T(8,128)(2,1)}), bf16[1024,3696]{1,0:T(8,128)(2,1)}) %all-gather.5.cloned.1.call-update) | async-done | bytes 7569424 | tf_op jit(solution)/shard_map/all_gather | solution.py:152
  449.8 9.6 %convolution_convert_fusion.2 = bf16[1024,512]{1,0:T(8,128)(2,1)} fusion(bf16[1024,3696]{1,0:T(8,128)(2,1)} %all-gather.5.cloned.1.call-done, bf16[3696,512]{1,0:T(8,128)(2,1)} %param.28), kind=kOutput, calls=%fused_computation.32 | convolution fusion | flops 3876061184 | bytes 12402688 | tf_op jit(solution)/shard_map/dot_general | solution.py:151
  459.4 75.1 %all-reduce.7.cloned.1.call-done = bf16[1024,512]{1,0:T(8,128)(2,1)} async-done(((bf16[1024,512]{1,0:T(8,128)(2,1)}), bf16[1024,512]{1,0:T(8,128)(2,1)}) %all-reduce.7.cloned.1.call-update) | async-done | bytes 1048592 | tf_op jit(solution)/shard_map/psum | solution.py:154
  534.5 2.5 fusion.19
  (64 shorter events, 3.8 us)
Async XLA Ops:
  6.5 83.4 %copy-start = (bf16[1,8192,1,128]{3,1,2,0:T(8,128)(2,1)S(1)}, bf16[1,8192,1,128]{3,1,2,0:T(8,128)(2,1)}, u32[]{:S(2)}) copy-start(bf16[1,8192,1,128]{3,1,2,0:T(8,128)(2,1)} %param.32) | copy-start | bytes 6291460
  6.5 81.8 %reduce-scatter.3.cloned.1.call-start = ((), (), s32[]{:S(2)}) async-start(), calls=%async_computation.2 | async-start | bytes 2785280 | tf_op jit(solution)/shard_map/reduce_scatter | solution.py:73
  7.4 4.9 copy-start.7
  7.4 4.9 copy-start.4
  7.4 4.9 copy-start.8
  7.4 5.5 %copy-start.2 = (bf16[1024,512]{1,0:T(8,128)(2,1)S(1)}, bf16[1024,512]{1,0:T(8,128)(2,1)}, u32[]{:S(2)}) copy-start(bf16[1024,512]{1,0:T(8,128)(2,1)} %param.20) | copy-start | bytes 3145732
  7.4 45.7 %copy-start.6 = (s32[64]{0:T(128)S(1)}, s32[64]{0:T(128)}, u32[]{:S(2)}) copy-start(s32[64]{0:T(128)} %param.31) | copy-start | bytes 772
  12.2 136.3 %all-gather.3.cloned.1.call-start = ((), (), s32[]{:S(2)}) async-start(), calls=%async_computation.3 | async-start | bytes 2228224 | tf_op jit(solution)/shard_map/all_gather | solution.py:123
  101.3 51.3 %copy-start.5 = (bf16[512]{0:T(512)(128)(2,1)S(1)}, bf16[512]{0:T(512)(128)(2,1)}, u32[]{:S(2)}) copy-start(bf16[512]{0:T(512)(128)(2,1)} %param.25) | copy-start | bytes 3076
  101.3 127.5 %copy-start.3 = (bf16[1024,512]{1,0:T(8,128)(2,1)S(1)}, bf16[1024,512]{1,0:T(8,128)(2,1)}, u32[]{:S(2)}) copy-start(bf16[1024,512]{1,0:T(8,128)(2,1)} %param.20) | copy-start | bytes 3145732
  101.3 127.4 %all-reduce.5.cloned.1.call-start = ((), (), s32[]{:S(2)}) async-start(), calls=%async_computation.4 | async-start | bytes 2097152 | tf_op jit(solution)/shard_map/psum | solution.py:127
  152.6 227.3 %reduce-scatter.5.cloned.1.call-start = ((), (), s32[]{:S(2)}) async-start(), calls=%async_computation.5 | async-start | bytes 16154624 | tf_op jit(solution)/shard_map/reduce_scatter | solution.py:141
  245.0 204.8 %all-gather.5.cloned.1.call-start = ((), (), s32[]{:S(2)}) async-start(), calls=%async_computation.6 | async-start | bytes 8077312 | tf_op jit(solution)/shard_map/all_gather | solution.py:152
  382.3 152.2 %all-reduce.7.cloned.1.call-start = ((), (), s32[]{:S(2)}) async-start(), calls=%async_computation.7 | async-start | bytes 2097152 | tf_op jit(solution)/shard_map/psum | solution.py:154
  449.8 87.2 %copy-start.1 = (bf16[1,8192,1,128]{3,1,2,0:T(8,128)(2,1)S(1)}, bf16[1,8192,1,128]{3,1,2,0:T(8,128)(2,1)}, u32[]{:S(2)}) copy-start(bf16[1,8192,1,128]{3,1,2,0:T(8,128)(2,1)} %param.32) | copy-start | bytes 6291460
Sparse Core Ops, SparseCore 0:
  12.3 75.9 reduce-scatter.2
  101.4 47.0 all-gather.2
  152.7 76.0 all-reduce.4
  245.1 134.6 reduce-scatter.4
  382.4 67.3 all-gather.4
  459.5 74.9 all-reduce.6

commit v2 on v1

--- a/solution.py
+++ b/solution.py
@@ -46,6 +46,17 @@
     return (total, summed)
 
 
+def kv_sum(part, base, kv_slot, n_kv):
+    rows = part.shape[0] // n_kv
+    got = lax.all_to_all(
+        part.astype(jnp.bfloat16).reshape(n_kv, rows, part.shape[1]), "kv", 0, 0, tiled=False
+    )
+    own = lax.dynamic_slice_in_dim(base, kv_slot * rows, rows, 0)
+    chunk = (own + jnp.sum(got.astype(jnp.float32), axis=0)).astype(jnp.bfloat16)
+    spread = jnp.broadcast_to(chunk[None], (n_kv,) + chunk.shape)
+    return lax.all_to_all(spread, "kv", 0, 0, tiled=False).reshape(part.shape)
+
+
 def per_device(
     tokens,
     norm_in,
@@ -68,15 +79,21 @@
     scale = HD ** (-0.5)
     wide = tokens.astype(jnp.float32)
     slot = lax.axis_index("req")
-    square_in = lax.psum(jnp.sum(wide * wide, axis=1), "req")
+    kv_slot = lax.axis_index("kv")
+    n_req = tokens.shape[0] // REQ_DEV
+    n_kv = lax.psum(1, "kv")
+    square_part = jnp.sum(wide * wide, axis=1)
+    square_hi = square_part.astype(jnp.bfloat16)
+    square_lo = (square_part - square_hi.astype(jnp.float32)).astype(jnp.bfloat16)
+    square_cols = jnp.pad(jnp.stack([square_hi, square_lo], axis=1), ((0, 0), (0, 126)))
     gained = (wide * norm_in.astype(jnp.float32)[None, :]).astype(jnp.bfloat16)
-    united = lax.psum_scatter(
-        jnp.dot(gained, w_qkv, preferred_element_type=jnp.float32).astype(jnp.bfloat16),
-        "req",
-        scatter_dimension=0,
-        tiled=True,
-    ).astype(jnp.float32)
-    scale_in = lax.rsqrt(lax.dynamic_slice_in_dim(square_in, slot * REQ_DEV, REQ_DEV) / D + EPS)
+    qkv_part = jnp.dot(gained, w_qkv, preferred_element_type=jnp.float32).astype(jnp.bfloat16)
+    width = qkv_part.shape[1]
+    sent = jnp.concatenate([qkv_part, square_cols], axis=1).reshape(n_req, REQ_DEV, width + 128)
+    got = lax.all_to_all(sent, "req", 0, 0, tiled=False).astype(jnp.float32)
+    united = jnp.sum(got[:, :, :width], axis=0)
+    square_in = jnp.sum(got[:, :, width] + got[:, :, width + 1], axis=0)
+    scale_in = lax.rsqrt(square_in / D + EPS)
     united = (united * scale_in[:, None] + qkv_bias.astype(jnp.float32)[None, :]).reshape(
         REQ_DEV, heads_here, GROUP + 2, HD
     )
@@ -124,8 +141,7 @@
         w_out,
         preferred_element_type=jnp.float32,
     )
-    projected = lax.psum(out_part.astype(jnp.bfloat16), "kv").astype(jnp.float32)
-    residual = lax.optimization_barrier((wide + projected).astype(jnp.bfloat16))
+    residual = kv_sum(out_part, wide, kv_slot, n_kv)
     resid_wide = residual.astype(jnp.float32)
     square_mid = lax.psum(jnp.sum(resid_wide * resid_wide, axis=1), "req")
     mixed_in = (resid_wide * norm_mid.astype(jnp.float32)[None, :]).astype(jnp.bfloat16)
@@ -151,8 +167,7 @@
     down_part = jnp.dot(
         lax.all_gather(act, "req", axis=0, tiled=True), w_down, preferred_element_type=jnp.float32
     )
-    down = lax.psum(down_part.astype(jnp.bfloat16), "kv").astype(jnp.float32)
-    return (resid_wide + down).astype(jnp.bfloat16)
+    return kv_sum(down_part, resid_wide, kv_slot, n_kv)
 
 
 def solution(mesh):

time: 544 us -> 446 us (0.82)
  waiting for transfers between devices: 402 us -> 280 us
  starting transfers between devices: 0.21 us -> 16.4 us
  other arithmetic: 11.2 us -> 17.9 us
    psum x2 -> x0, waiting for transfers between devices: 151 us -> none  [the longest x1 76.1 us: per_device(): lax.psum(out_part.astype(jnp.bfloat16), 'kv').astype(jnp.float32)]
    all_to_all x0 -> x3, waiting for transfers between devices: none -> 66 us  [the longest x1 36 us: per_device(): got = lax.all_to_all(sent, 'req', 0, 0, tiled=False).astype(jnp.float32)]
    psum x1 -> x0, blocking collectives: 39.1 us -> none  [per_device(): square_in = lax.psum(jnp.sum(wide * wide, axis=1), 'req')]
    all_to_all x0 -> x2, blocking collectives: none -> 38.7 us  [the longest x1 20.4 us: kv_sum(): lax.all_to_all(part.astype(jnp.bfloat16).reshape(n_kv, rows, part.shape[1...]
    reduce_scatter x1 -> x0, waiting for transfers between devices: 35 us -> none  [per_device(): lax.psum_scatter(jnp.dot(gained, w_qkv, preferred_element_type=jnp.float3...]
    all_to_all x0 -> x3, starting transfers between devices: none -> 16.1 us  [the longest x1 8.19 us: per_device(): got = lax.all_to_all(sent, 'req', 0, 0, tiled=False).astype(jnp.float32)]
  transfers between devices with their start and end apart: 6 -> 6, of which waited for: 6 -> 6; matrix products, arithmetic and copies ran while one was open for 0% -> 1% of each run, Pallas kernels for 0% -> 0%
where the time goes in v2:
time: 446 us
  waiting for transfers between devices  280 us (63%)
  blocking collectives  75 us (17%)
  matrix products  38.1 us (9%)
  other arithmetic  17.9 us (4%)
  starting transfers between devices  16.4 us (4%)
  between operations  13.5 us (3%)
    reduce_scatter x1, waiting for transfers between devices, per_device(): lax.psum_scatter(jnp.dot(mixed_in, w_gate_up, preferred_element_type=jnp....  95.9 us
    all_gather x1, waiting for transfers between devices, per_device(): lax.all_gather(act, 'req', axis=0, tiled=True)  67.5 us
    all_gather x1, waiting for transfers between devices, per_device(): lax.all_gather(attended, 'req', axis=0, tiled=True)  50.9 us
    psum x1, blocking collectives, per_device(): square_mid = lax.psum(jnp.sum(resid_wide * resid_wide, axis=1), 'req')  36.3 us
    all_to_all x1, waiting for transfers between devices, per_device(): got = lax.all_to_all(sent, 'req', 0, 0, tiled=False).astype(jnp.float32)  36 us
    all_to_all x1, blocking collectives, kv_sum(): lax.all_to_all(part.astype(jnp.bfloat16).reshape(n_kv, rows, part.shape[1...  20.4 us
    all_to_all x1, blocking collectives, kv_sum(): return lax.all_to_all(spread, 'kv', 0, 0, tiled=False).reshape(part.shape)  18.3 us
    all_to_all x1, waiting for transfers between devices, kv_sum(): return lax.all_to_all(spread, 'kv', 0, 0, tiled=False).reshape(part.shape)  15.6 us
  transfers between devices with their start and end apart: 6, of which 6 were waited for; matrix products, arithmetic and copies ran while one was open for 1% of the time, Pallas kernels for 0%

profile of v2, /device:TPU:0, one launch (start us, length us, event | category | flops | bytes accessed | tf_op | source)
XLA Modules:
  0.0 445.6 jit_solution(15129756225329363149)
XLA Ops:
  6.5 1.6 multiply_reduce_fusion.1
  9.1 3.2 convolution_convert_fusion.1
  12.3 1.8 fusion.15
  14.1 8.2 %all-to-all-start = ((bf16[16,64,1408]{2,1,0:T(8,128)(2,1)}), bf16[16,64,1408]{2,1,0:T(8,128)(2,1)}, u32[]{:S(2)}, u32[]{:S(2)}) async-start(bf16[16,64,1408]{2,1,0:T(8,128)(2,1)} %bitcast.94), calls=%async_computation | async-start | bytes 5767168 | tf_op jit(solution)/shard_map/all_to_all | solution.py:93
  24.0 36.0 %all-to-all-done = bf16[16,64,1408]{2,1,0:T(8,128)(2,1)} async-done(((bf16[16,64,1408]{2,1,0:T(8,128)(2,1)}), bf16[16,64,1408]{2,1,0:T(8,128)(2,1)}, u32[]{:S(2)}, u32[]{:S(2)}) %all-to-all-start) | async-done | bytes 2883616 | tf_op jit(solution)/shard_map/all_to_all | solution.py:93
  60.1 2.4 convert_element_type.142
  67.6 2.9 fusion.25
  70.5 2.0 fusion.34
  73.4 50.9 %all-gather.3.cloned.1.call-done = bf16[1024,1024]{1,0:T(8,128)(2,1)} async-done(((bf16[64,1024]{1,0:T(8,128)(2,1)}), bf16[1024,1024]{1,0:T(8,128)(2,1)}) %all-gather.3.cloned.1.call-update) | async-done | bytes 2097168 | tf_op jit(solution)/shard_map/all_gather | solution.py:140
  124.3 4.1 convolution_convert_fusion.3
  128.3 4.4 all-to-all-start.1
  132.7 1.6 convert_element_type.135
  134.4 14.4 %all-to-all-done.1 = bf16[8,128,512]{2,1,0:T(8,128)(2,1)S(1)} async-done(((bf16[8,128,512]{2,1,0:T(8,128)(2,1)}), bf16[8,128,512]{2,1,0:T(8,128)(2,1)S(1)}, u32[]{:S(2)}, u32[]{:S(2)}) %all-to-all-start.1) | async-done | bytes 1048608 | tf_op jit(solution)/shard_map/all_to_all | solution.py:51
  151.0 3.6 all-to-all-start.2
  154.8 15.6 %all-to-all-done.2 = bf16[8,128,512]{2,1,0:T(8,128)(2,1)S(1)} async-done(((bf16[8,128,512]{2,1,0:T(8,128)(2,1)}), bf16[8,128,512]{2,1,0:T(8,128)(2,1)S(1)}, u32[]{:S(2)}, u32[]{:S(2)}) %all-to-all-start.2) | async-done | bytes 1048608 | tf_op jit(solution)/shard_map/all_to_all | solution.py:57
  170.3 1.7 bitcast_convert_fusion.1
  172.0 15.1 %convolution_convert_fusion = bf16[1024,7424]{1,0:T(8,128)(2,1)} fusion(bf16[512,3696]{0,1:T(8,128)(2,1)} %param.27, bf16[512,3696]{0,1:T(8,128)(2,1)} %param.26, f32[1024,512]{1,0:T(8,128)} %bitcast_convert_fusion.1, f32[512]{0:T(512)S(1)} %convert_element_type.153), kind=kOutput, calls=%fused_computation.4 | convolution fusion | flops 7823687680 | bytes 24872960 | tf_op jit(solution)/shard_map/dot_general | solution.py:158
  187.5 36.3 %psum.7 = f32[1024]{0:T(1024)S(1)} all-reduce(f32[1024]{0:T(1024)S(1)} %bitcast.110), channel_id=1, replica_groups=mesh['req'=16,'kv'=8] {'req'}, use_global_device_ids=true, to_apply=%region_10.11 | all-reduce | flops 1024 | bytes 8192 | tf_op jit(solution)/shard_map/psum | solution.py:146
  223.9 95.9 %reduce-scatter.2.cloned.1.call-done = bf16[64,7424]{1,0:T(8,128)(2,1)} async-done(((bf16[1024,7424]{1,0:T(8,128)(2,1)}), bf16[64,7424]{1,0:T(8,128)(2,1)}) %reduce-scatter.2.cloned.1.call-update) | async-done | bytes 950288 | tf_op jit(solution)/shard_map/reduce_scatter | solution.py:157
  319.8 1.3 convert_element_type.156
  322.2 67.5 %all-gather.5.cloned.1.call-done = bf16[1024,3696]{1,0:T(8,128)(2,1)} async-done(((bf16[64,3696]{1,0:T(8,128)(2,1)}), bf16[1024,3696]{1,0:T(8,128)(2,1)}) %all-gather.5.cloned.1.call-update) | async-done | bytes 7569424 | tf_op jit(solution)/shard_map/all_gather | solution.py:168
  389.8 8.4 %convolution_convert_fusion.2 = bf16[1024,512]{1,0:T(8,128)(2,1)S(1)} fusion(bf16[1024,3696]{1,0:T(8,128)(2,1)} %all-gather.5.cloned.1.call-done, bf16[3696,512]{1,0:T(8,128)(2,1)} %param.28), kind=kOutput, calls=%fused_computation.30 | convolution fusion | flops 3876061184 | bytes 12402688 | tf_op jit(solution)/shard_map/dot_general | solution.py:167
  398.2 20.4 %all_to_all.25 = bf16[8,128,512]{2,1,0:T(8,128)(2,1)S(1)} all-to-all(bf16[8,128,512]{2,1,0:T(8,128)(2,1)S(1)} %bitcast.101), channel_id=1, replica_groups=mesh['req'=16,'kv'=8] {'kv'}, dimensions={0} | all-to-all | bytes 2097152 | tf_op jit(solution)/shard_map/all_to_all | solution.py:51
  419.8 18.3 %all_to_all.26 = bf16[8,128,512]{2,1,0:T(8,128)(2,1)S(1)} all-to-all(bf16[8,128,512]{2,1,0:T(8,128)(2,1)S(1)} %broadcast_in_dim.40), channel_id=1, replica_groups=mesh['req'=16,'kv'=8] {'kv'}, dimensions={0} | all-to-all | bytes 2097152 | tf_op jit(solution)/shard_map/all_to_all | solution.py:57
  (77 shorter events, 14.5 us)
Async XLA Ops:
  6.5 57.2 %copy-start = (bf16[1,8192,1,128]{3,1,2,0:T(8,128)(2,1)S(1)}, bf16[1,8192,1,128]{3,1,2,0:T(8,128)(2,1)}, u32[]{:S(2)}) copy-start(bf16[1,8192,1,128]{3,1,2,0:T(8,128)(2,1)} %param.32) | copy-start | bytes 6291460
  14.1 8.3 %copy-start.7 = (s32[64]{0:T(128)S(1)}, s32[64]{0:T(128)}, u32[]{:S(2)}) copy-start(s32[64]{0:T(128)} %param.35) | copy-start | bytes 772
  14.1 8.3 %copy-start.8 = (s32[16]{0:T(128)S(1)}, s32[16]{0:T(128)}, u32[]{:S(2)}) copy-start(s32[16]{0:T(128)} %param.34) | copy-start | bytes 196
  14.1 9.6 %copy-start.4 = (bf16[1280]{0:T(1024)(128)(2,1)S(1)}, bf16[1280]{0:T(1024)(128)(2,1)}, u32[]{:S(2)}) copy-start(bf16[1280]{0:T(1024)(128)(2,1)} %param.23) | copy-start | bytes 7684
  14.1 9.6 %copy-start.6 = (s32[64]{0:T(128)S(1)}, s32[64]{0:T(128)}, u32[]{:S(2)}) copy-start(s32[64]{0:T(128)} %param.31) | copy-start | bytes 772
  14.1 45.9 %all-to-all-start = ((bf16[16,64,1408]{2,1,0:T(8,128)(2,1)}), bf16[16,64,1408]{2,1,0:T(8,128)(2,1)}, u32[]{:S(2)}, u32[]{:S(2)}) async-start(bf16[16,64,1408]{2,1,0:T(8,128)(2,1)} %bitcast.94), calls=%async_computation | async-start | bytes 5767168 | tf_op jit(solution)/shard_map/all_to_all | solution.py:93
  22.3 101.9 %all-gather.3.cloned.1.call-start = ((), (), s32[]{:S(2)}) async-start(), calls=%async_computation.6 | async-start | bytes 2228224 | tf_op jit(solution)/shard_map/all_gather | solution.py:140
  63.1 2.2 copy-start.3
  73.4 59.3 %copy-start.2 = (bf16[1024,512]{1,0:T(8,128)(2,1)S(1)}, bf16[1024,512]{1,0:T(8,128)(2,1)}, u32[]{:S(2)}) copy-start(bf16[1024,512]{1,0:T(8,128)(2,1)} %param.20) | copy-start | bytes 3145732
  128.3 20.4 %all-to-all-start.1 = ((bf16[8,128,512]{2,1,0:T(8,128)(2,1)}), bf16[8,128,512]{2,1,0:T(8,128)(2,1)S(1)}, u32[]{:S(2)}, u32[]{:S(2)}) async-start(bf16[8,128,512]{2,1,0:T(8,128)(2,1)} %bitcast.29), calls=%async_computation.1 | async-start | bytes 2097152 | tf_op jit(solution)/shard_map/all_to_all | solution.py:51
  132.7 22.1 %copy-start.5 = (bf16[512]{0:T(512)(128)(2,1)S(1)}, bf16[512]{0:T(512)(128)(2,1)}, u32[]{:S(2)}) copy-start(bf16[512]{0:T(512)(128)(2,1)} %param.25) | copy-start | bytes 3076
  151.0 19.4 %all-to-all-start.2 = ((bf16[8,128,512]{2,1,0:T(8,128)(2,1)}), bf16[8,128,512]{2,1,0:T(8,128)(2,1)S(1)}, u32[]{:S(2)}, u32[]{:S(2)}) async-start(bf16[8,128,512]{2,1,0:T(8,128)(2,1)} %broadcast_in_dim.39), calls=%async_computation.2 | async-start | bytes 2097152 | tf_op jit(solution)/shard_map/all_to_all | solution.py:57
  154.5 165.2 %reduce-scatter.2.cloned.1.call-start = ((), (), s32[]{:S(2)}) async-start(), calls=%async_computation.7 | async-start | bytes 16154624 | tf_op jit(solution)/shard_map/reduce_scatter | solution.py:157
  187.2 202.6 %all-gather.5.cloned.1.call-start = ((), (), s32[]{:S(2)}) async-start(), calls=%async_computation.8 | async-start | bytes 8077312 | tf_op jit(solution)/shard_map/all_gather | solution.py:168
  398.2 40.9 %copy-start.1 = (bf16[1,8192,1,128]{3,1,2,0:T(8,128)(2,1)S(1)}, bf16[1,8192,1,128]{3,1,2,0:T(8,128)(2,1)}, u32[]{:S(2)}) copy-start(bf16[1,8192,1,128]{3,1,2,0:T(8,128)(2,1)} %param.32) | copy-start | bytes 6291460
Sparse Core Ops, SparseCore 0:
  73.5 50.7 all-gather.2
  187.3 132.4 reduce-scatter.1
  322.3 67.3 all-gather.4

commit v3 on v2

--- a/solution.py
+++ b/solution.py
@@ -137,7 +137,9 @@
         (summed / total[..., None]).astype(jnp.bfloat16).reshape(REQ_DEV, heads_here * GROUP * HD)
     )
     out_part = jnp.dot(
-        lax.all_gather(attended, "req", axis=0, tiled=True),
+        lax.all_to_all(
+            jnp.broadcast_to(attended[None], (n_req,) + attended.shape), "req", 0, 0, tiled=False
+        ).reshape(n_req * REQ_DEV, attended.shape[1]),
         w_out,
         preferred_element_type=jnp.float32,
     )

time: 446 us -> 429 us (0.962)
  waiting for transfers between devices: 280 us -> 229 us
  blocking collectives: 75 us -> 110 us
    all_gather x1 -> x0, waiting for transfers between devices: 50.9 us -> none  [per_device(): lax.all_gather(attended, 'req', axis=0, tiled=True)]
    all_to_all x0 -> x1, blocking collectives: none -> 36.9 us  [per_device(): lax.all_to_all(jnp.broadcast_to(attended[None], (n_req,) + attended.shape...]
  transfers between devices with their start and end apart: 6 -> 5, of which waited for: 6 -> 5; matrix products, arithmetic and copies ran while one was open for 1% -> 1% of each run, Pallas kernels for 0% -> 0%
where the time goes in v3:
time: 429 us; the launch traced here: 428 us
  waiting for transfers between devices  229 us (53%)
  blocking collectives  110 us (26%)
  matrix products  36.2 us (8%)
  other arithmetic  17.9 us (4%)
  starting transfers between devices  16.8 us (4%)
  between operations  13.8 us (3%)
    reduce_scatter x1, waiting for transfers between devices, per_device(): lax.psum_scatter(jnp.dot(mixed_in, w_gate_up, preferred_element_type=jnp....  96.6 us
    all_gather x1, waiting for transfers between devices, per_device(): lax.all_gather(act, 'req', axis=0, tiled=True)  67.6 us
    all_to_all x1, blocking collectives, per_device(): lax.all_to_all(jnp.broadcast_to(attended[None], (n_req,) + attended.shape...  36.9 us
    all_to_all x1, waiting for transfers between devices, per_device(): got = lax.all_to_all(sent, 'req', 0, 0, tiled=False).astype(jnp.float32)  36.1 us
    psum x1, blocking collectives, per_device(): square_mid = lax.psum(jnp.sum(resid_wide * resid_wide, axis=1), 'req')  34.4 us
    all_to_all x1, blocking collectives, kv_sum(): lax.all_to_all(part.astype(jnp.bfloat16).reshape(n_kv, rows, part.shape[1...  20.4 us
    all_to_all x1, blocking collectives, kv_sum(): return lax.all_to_all(spread, 'kv', 0, 0, tiled=False).reshape(part.shape)  18.3 us
    all_to_all x1, waiting for transfers between devices, kv_sum(): return lax.all_to_all(spread, 'kv', 0, 0, tiled=False).reshape(part.shape)  15.6 us
  transfers between devices with their start and end apart: 5, of which 5 were waited for; matrix products, arithmetic and copies ran while one was open for 1% of the time, Pallas kernels for 0%

profile of v3, /device:TPU:0, one launch (start us, length us, event | category | flops | bytes accessed | tf_op | source)
XLA Modules:
  0.0 428.1 jit_solution(5118760920356183715)
XLA Ops:
  6.5 1.6 multiply_reduce_fusion.1
  9.1 3.2 convolution_convert_fusion.1
  12.3 1.8 fusion.15
  14.1 8.2 %all-to-all-start = ((bf16[16,64,1408]{2,1,0:T(8,128)(2,1)}), bf16[16,64,1408]{2,1,0:T(8,128)(2,1)}, u32[]{:S(2)}, u32[]{:S(2)}) async-start(bf16[16,64,1408]{2,1,0:T(8,128)(2,1)} %bitcast.95), calls=%async_computation | async-start | bytes 5767168 | tf_op jit(solution)/shard_map/all_to_all | solution.py:93
  24.0 36.1 %all-to-all-done = bf16[16,64,1408]{2,1,0:T(8,128)(2,1)} async-done(((bf16[16,64,1408]{2,1,0:T(8,128)(2,1)}), bf16[16,64,1408]{2,1,0:T(8,128)(2,1)}, u32[]{:S(2)}, u32[]{:S(2)}) %all-to-all-start) | async-done | bytes 2883616 | tf_op jit(solution)/shard_map/all_to_all | solution.py:93
  60.1 2.4 convert_element_type.142
  67.6 2.9 fusion.25
  70.5 2.0 fusion.34
  73.0 36.9 %all_to_all.30 = bf16[16,64,1024]{2,1,0:T(8,128)(2,1)S(1)} all-to-all(bf16[16,64,1024]{2,1,0:T(8,128)(2,1)S(1)} %broadcast_in_dim.44), channel_id=1, replica_groups=mesh['req'=16,'kv'=8] {'req'}, dimensions={0} | all-to-all | bytes 4194304 | tf_op jit(solution)/shard_map/all_to_all | solution.py:140
  109.9 2.2 convolution_convert_fusion.3
  112.1 4.8 %all-to-all-start.2 = ((bf16[8,128,512]{2,1,0:T(8,128)(2,1)}), bf16[8,128,512]{2,1,0:T(8,128)(2,1)S(1)}, u32[]{:S(2)}, u32[]{:S(2)}) async-start(bf16[8,128,512]{2,1,0:T(8,128)(2,1)} %bitcast.30), calls=%async_computation.2 | async-start | bytes 2097152 | tf_op jit(solution)/shard_map/all_to_all | solution.py:51
  116.9 1.6 convert_element_type.135
  118.5 13.5 %all-to-all-done.2 = bf16[8,128,512]{2,1,0:T(8,128)(2,1)S(1)} async-done(((bf16[8,128,512]{2,1,0:T(8,128)(2,1)}), bf16[8,128,512]{2,1,0:T(8,128)(2,1)S(1)}, u32[]{:S(2)}, u32[]{:S(2)}) %all-to-all-start.2) | async-done | bytes 1048608 | tf_op jit(solution)/shard_map/all_to_all | solution.py:51
  134.2 3.6 all-to-all-start.3
  138.1 15.6 %all-to-all-done.3 = bf16[8,128,512]{2,1,0:T(8,128)(2,1)S(1)} async-done(((bf16[8,128,512]{2,1,0:T(8,128)(2,1)}), bf16[8,128,512]{2,1,0:T(8,128)(2,1)S(1)}, u32[]{:S(2)}, u32[]{:S(2)}) %all-to-all-start.3) | async-done | bytes 1048608 | tf_op jit(solution)/shard_map/all_to_all | solution.py:57
  153.6 1.7 bitcast_convert_fusion.1
  155.3 15.1 %convolution_convert_fusion = bf16[1024,7424]{1,0:T(8,128)(2,1)} fusion(bf16[512,3696]{0,1:T(8,128)(2,1)} %param.27, bf16[512,3696]{0,1:T(8,128)(2,1)} %param.26, f32[1024,512]{1,0:T(8,128)} %bitcast_convert_fusion.1, f32[512]{0:T(512)S(1)} %convert_element_type.153), kind=kOutput, calls=%fused_computation.4 | convolution fusion | flops 7823687680 | bytes 24872960 | tf_op jit(solution)/shard_map/dot_general | solution.py:160
  170.7 34.4 %psum.7 = f32[1024]{0:T(1024)S(1)} all-reduce(f32[1024]{0:T(1024)S(1)} %bitcast.112), channel_id=1, replica_groups=mesh['req'=16,'kv'=8] {'req'}, use_global_device_ids=true, to_apply=%region_10.11 | all-reduce | flops 1024 | bytes 8192 | tf_op jit(solution)/shard_map/psum | solution.py:148
  205.2 96.6 %reduce-scatter.2.cloned.1.call-done = bf16[64,7424]{1,0:T(8,128)(2,1)} async-done(((bf16[1024,7424]{1,0:T(8,128)(2,1)}), bf16[64,7424]{1,0:T(8,128)(2,1)}) %reduce-scatter.2.cloned.1.call-update) | async-done | bytes 950288 | tf_op jit(solution)/shard_map/reduce_scatter | solution.py:159
  301.9 1.3 convert_element_type.156
  304.3 67.6 %all-gather.2.cloned.1.call-done = bf16[1024,3696]{1,0:T(8,128)(2,1)} async-done(((bf16[64,3696]{1,0:T(8,128)(2,1)}), bf16[1024,3696]{1,0:T(8,128)(2,1)}) %all-gather.2.cloned.1.call-update) | async-done | bytes 7569424 | tf_op jit(solution)/shard_map/all_gather | solution.py:170
  371.9 8.4 %convolution_convert_fusion.2 = bf16[1024,512]{1,0:T(8,128)(2,1)S(1)} fusion(bf16[1024,3696]{1,0:T(8,128)(2,1)} %all-gather.2.cloned.1.call-done, bf16[3696,512]{1,0:T(8,128)(2,1)} %param.28), kind=kOutput, calls=%fused_computation.30 | convolution fusion | flops 3876061184 | bytes 12402688 | tf_op jit(solution)/shard_map/dot_general | solution.py:169
  380.4 20.4 %all_to_all.31 = bf16[8,128,512]{2,1,0:T(8,128)(2,1)S(1)} all-to-all(bf16[8,128,512]{2,1,0:T(8,128)(2,1)S(1)} %bitcast.103), channel_id=1, replica_groups=mesh['req'=16,'kv'=8] {'kv'}, dimensions={0} | all-to-all | bytes 2097152 | tf_op jit(solution)/shard_map/all_to_all | solution.py:51
  402.0 18.3 %all_to_all.32 = bf16[8,128,512]{2,1,0:T(8,128)(2,1)S(1)} all-to-all(bf16[8,128,512]{2,1,0:T(8,128)(2,1)S(1)} %broadcast_in_dim.76), channel_id=1, replica_groups=mesh['req'=16,'kv'=8] {'kv'}, dimensions={0} | all-to-all | bytes 2097152 | tf_op jit(solution)/shard_map/all_to_all | solution.py:57
  (78 shorter events, 14.0 us)
Async XLA Ops:
  6.5 57.2 %copy-start = (bf16[1,8192,1,128]{3,1,2,0:T(8,128)(2,1)S(1)}, bf16[1,8192,1,128]{3,1,2,0:T(8,128)(2,1)}, u32[]{:S(2)}) copy-start(bf16[1,8192,1,128]{3,1,2,0:T(8,128)(2,1)} %param.32) | copy-start | bytes 6291460
  14.1 8.2 %copy-start.8 = (s32[64]{0:T(128)S(1)}, s32[64]{0:T(128)}, u32[]{:S(2)}) copy-start(s32[64]{0:T(128)} %param.35) | copy-start | bytes 772
  14.1 8.2 %copy-start.9 = (s32[16]{0:T(128)S(1)}, s32[16]{0:T(128)}, u32[]{:S(2)}) copy-start(s32[16]{0:T(128)} %param.34) | copy-start | bytes 196
  14.1 9.5 %copy-start.4 = (bf16[1280]{0:T(1024)(128)(2,1)S(1)}, bf16[1280]{0:T(1024)(128)(2,1)}, u32[]{:S(2)}) copy-start(bf16[1280]{0:T(1024)(128)(2,1)} %param.23) | copy-start | bytes 7684
  14.1 9.5 %copy-start.6 = (s32[64]{0:T(128)S(1)}, s32[64]{0:T(128)}, u32[]{:S(2)}) copy-start(s32[64]{0:T(128)} %param.31) | copy-start | bytes 772
  14.1 45.9 %all-to-all-start = ((bf16[16,64,1408]{2,1,0:T(8,128)(2,1)}), bf16[16,64,1408]{2,1,0:T(8,128)(2,1)}, u32[]{:S(2)}, u32[]{:S(2)}) async-start(bf16[16,64,1408]{2,1,0:T(8,128)(2,1)} %bitcast.95), calls=%async_computation | async-start | bytes 5767168 | tf_op jit(solution)/shard_map/all_to_all | solution.py:93
  63.1 2.2 copy-start.3
  72.5 37.4 %copy-start.7 = (bf16[1024,512]{1,0:T(8,128)(2,1)S(1)}, bf16[1024,512]{1,0:T(8,128)(2,1)}, u32[]{:S(2)}) copy-start(bf16[1024,512]{1,0:T(8,128)(2,1)} %param.24) | copy-start | bytes 3145732
  109.9 7.0 %copy-start.2 = (bf16[1024,512]{1,0:T(8,128)(2,1)S(1)}, bf16[1024,512]{1,0:T(8,128)(2,1)}, u32[]{:S(2)}) copy-start(bf16[1024,512]{1,0:T(8,128)(2,1)} %param.20) | copy-start | bytes 3145732
  112.1 19.9 %all-to-all-start.2 = ((bf16[8,128,512]{2,1,0:T(8,128)(2,1)}), bf16[8,128,512]{2,1,0:T(8,128)(2,1)S(1)}, u32[]{:S(2)}, u32[]{:S(2)}) async-start(bf16[8,128,512]{2,1,0:T(8,128)(2,1)} %bitcast.30), calls=%async_computation.2 | async-start | bytes 2097152 | tf_op jit(solution)/shard_map/all_to_all | solution.py:51
  116.9 21.1 %copy-start.5 = (bf16[512]{0:T(512)(128)(2,1)S(1)}, bf16[512]{0:T(512)(128)(2,1)}, u32[]{:S(2)}) copy-start(bf16[512]{0:T(512)(128)(2,1)} %param.25) | copy-start | bytes 3076
  134.2 19.4 %all-to-all-start.3 = ((bf16[8,128,512]{2,1,0:T(8,128)(2,1)}), bf16[8,128,512]{2,1,0:T(8,128)(2,1)S(1)}, u32[]{:S(2)}, u32[]{:S(2)}) async-start(bf16[8,128,512]{2,1,0:T(8,128)(2,1)} %broadcast_in_dim.45), calls=%async_computation.3 | async-start | bytes 2097152 | tf_op jit(solution)/shard_map/all_to_all | solution.py:57
  137.8 164.1 %reduce-scatter.2.cloned.1.call-start = ((), (), s32[]{:S(2)}) async-start(), calls=%async_computation.7 | async-start | bytes 16154624 | tf_op jit(solution)/shard_map/reduce_scatter | solution.py:159
  170.4 201.5 %all-gather.2.cloned.1.call-start = ((), (), s32[]{:S(2)}) async-start(), calls=%async_computation.8 | async-start | bytes 8077312 | tf_op jit(solution)/shard_map/all_gather | solution.py:170
  380.3 40.9 %copy-start.1 = (bf16[1,8192,1,128]{3,1,2,0:T(8,128)(2,1)S(1)}, bf16[1,8192,1,128]{3,1,2,0:T(8,128)(2,1)}, u32[]{:S(2)}) copy-start(bf16[1,8192,1,128]{3,1,2,0:T(8,128)(2,1)} %param.32) | copy-start | bytes 6291460
Sparse Core Ops, SparseCore 0:
  170.5 131.2 reduce-scatter.1
  304.4 67.4 all-gather.1

commit v4 on v3

--- a/solution.py
+++ b/solution.py
@@ -52,7 +52,7 @@
         part.astype(jnp.bfloat16).reshape(n_kv, rows, part.shape[1]), "kv", 0, 0, tiled=False
     )
     own = lax.dynamic_slice_in_dim(base, kv_slot * rows, rows, 0)
-    chunk = (own + jnp.sum(got.astype(jnp.float32), axis=0)).astype(jnp.bfloat16)
+    chunk = (own + jnp.sum(got, axis=0, dtype=jnp.float32)).astype(jnp.bfloat16)
     spread = jnp.broadcast_to(chunk[None], (n_kv,) + chunk.shape)
     return lax.all_to_all(spread, "kv", 0, 0, tiled=False).reshape(part.shape)
 
@@ -90,9 +90,9 @@
     qkv_part = jnp.dot(gained, w_qkv, preferred_element_type=jnp.float32).astype(jnp.bfloat16)
     width = qkv_part.shape[1]
     sent = jnp.concatenate([qkv_part, square_cols], axis=1).reshape(n_req, REQ_DEV, width + 128)
-    got = lax.all_to_all(sent, "req", 0, 0, tiled=False).astype(jnp.float32)
-    united = jnp.sum(got[:, :, :width], axis=0)
-    square_in = jnp.sum(got[:, :, width] + got[:, :, width + 1], axis=0)
+    got = lax.all_to_all(sent, "req", 0, 0, tiled=False)
+    united = jnp.sum(got[:, :, :width], axis=0, dtype=jnp.float32)
+    square_in = jnp.sum(got[:, :, width : width + 2], axis=(0, 2), dtype=jnp.float32)
     scale_in = lax.rsqrt(square_in / D + EPS)
     united = (united * scale_in[:, None] + qkv_bias.astype(jnp.float32)[None, :]).reshape(
         REQ_DEV, heads_here, GROUP + 2, HD
@@ -161,10 +161,10 @@
         "req",
         scatter_dimension=0,
         tiled=True,
-    ).astype(jnp.float32)
+    )
     scale_mid = lax.rsqrt(lax.dynamic_slice_in_dim(square_mid, slot * REQ_DEV, REQ_DEV) / D + EPS)
-    gate = gate_up[:, :units] * scale_mid[:, None]
-    up = gate_up[:, padded : padded + units] * scale_mid[:, None]
+    gate = gate_up[:, :units].astype(jnp.float32) * scale_mid[:, None]
+    up = gate_up[:, padded : padded + units].astype(jnp.float32) * scale_mid[:, None]
     act = (jax.nn.silu(gate) * up).astype(jnp.bfloat16)
     down_part = jnp.dot(
         lax.all_gather(act, "req", axis=0, tiled=True), w_down, preferred_element_type=jnp.float32

time: 429 us -> 429 us (level)
  no operation moved by 1% of the time
where the time goes in v4:
time: 429 us; the launch traced here: 428 us
  waiting for transfers between devices  229 us (53%)
  blocking collectives  110 us (26%)
  matrix products  36.2 us (8%)
  other arithmetic  18.2 us (4%)
  starting transfers between devices  16.8 us (4%)
  between operations  13.8 us (3%)
    reduce_scatter x1, waiting for transfers between devices, per_device(): lax.psum_scatter(jnp.dot(mixed_in, w_gate_up, preferred_element_type=jnp....  96.7 us
    all_gather x1, waiting for transfers between devices, per_device(): lax.all_gather(act, 'req', axis=0, tiled=True)  67.5 us
    all_to_all x1, blocking collectives, per_device(): lax.all_to_all(jnp.broadcast_to(attended[None], (n_req,) + attended.shape...  37.1 us
    all_to_all x1, waiting for transfers between devices, per_device(): got = lax.all_to_all(sent, 'req', 0, 0, tiled=False)  36.1 us
    psum x1, blocking collectives, per_device(): square_mid = lax.psum(jnp.sum(resid_wide * resid_wide, axis=1), 'req')  34.4 us
    all_to_all x1, blocking collectives, kv_sum(): lax.all_to_all(part.astype(jnp.bfloat16).reshape(n_kv, rows, part.shape[1...  20.2 us
    all_to_all x1, blocking collectives, kv_sum(): return lax.all_to_all(spread, 'kv', 0, 0, tiled=False).reshape(part.shape)  18.3 us
    all_to_all x1, waiting for transfers between devices, kv_sum(): return lax.all_to_all(spread, 'kv', 0, 0, tiled=False).reshape(part.shape)  15.6 us
  transfers between devices with their start and end apart: 5, of which 5 were waited for; matrix products, arithmetic and copies ran while one was open for 1% of the time, Pallas kernels for 0%

profile of v4, /device:TPU:0, one launch (start us, length us, event | category | flops | bytes accessed | tf_op | source)
XLA Modules:
  0.0 428.3 jit_solution(9500113246755418501)
XLA Ops:
  6.5 1.6 multiply_reduce_fusion.1
  9.1 3.2 convolution_convert_fusion.1
  12.3 1.8 fusion.15
  14.1 8.2 %all-to-all-start = ((bf16[16,64,1408]{2,1,0:T(8,128)(2,1)}), bf16[16,64,1408]{2,1,0:T(8,128)(2,1)}, u32[]{:S(2)}, u32[]{:S(2)}) async-start(bf16[16,64,1408]{2,1,0:T(8,128)(2,1)} %bitcast.95), calls=%async_computation | async-start | bytes 5767168 | tf_op jit(solution)/shard_map/all_to_all | solution.py:93
  24.0 36.1 %all-to-all-done = bf16[16,64,1408]{2,1,0:T(8,128)(2,1)} async-done(((bf16[16,64,1408]{2,1,0:T(8,128)(2,1)}), bf16[16,64,1408]{2,1,0:T(8,128)(2,1)}, u32[]{:S(2)}, u32[]{:S(2)}) %all-to-all-start) | async-done | bytes 2883616 | tf_op jit(solution)/shard_map/all_to_all | solution.py:93
  61.2 2.1 convert_reduce_fusion
  67.8 2.9 fusion.25
  70.8 2.0 fusion.34
  73.3 37.1 %all_to_all.30 = bf16[16,64,1024]{2,1,0:T(8,128)(2,1)S(1)} all-to-all(bf16[16,64,1024]{2,1,0:T(8,128)(2,1)S(1)} %broadcast_in_dim.44), channel_id=1, replica_groups=mesh['req'=16,'kv'=8] {'req'}, dimensions={0} | all-to-all | bytes 4194304 | tf_op jit(solution)/shard_map/all_to_all | solution.py:140
  110.3 2.2 convolution_convert_fusion.3
  112.5 4.8 %all-to-all-start.2 = ((bf16[8,128,512]{2,1,0:T(8,128)(2,1)}), bf16[8,128,512]{2,1,0:T(8,128)(2,1)S(1)}, u32[]{:S(2)}, u32[]{:S(2)}) async-start(bf16[8,128,512]{2,1,0:T(8,128)(2,1)} %bitcast.30), calls=%async_computation.2 | async-start | bytes 2097152 | tf_op jit(solution)/shard_map/all_to_all | solution.py:51
  117.3 1.6 convert_element_type.141
  119.0 13.5 %all-to-all-done.2 = bf16[8,128,512]{2,1,0:T(8,128)(2,1)S(1)} async-done(((bf16[8,128,512]{2,1,0:T(8,128)(2,1)}), bf16[8,128,512]{2,1,0:T(8,128)(2,1)S(1)}, u32[]{:S(2)}, u32[]{:S(2)}) %all-to-all-start.2) | async-done | bytes 1048608 | tf_op jit(solution)/shard_map/all_to_all | solution.py:51
  134.7 3.6 all-to-all-start.3
  138.5 15.6 %all-to-all-done.3 = bf16[8,128,512]{2,1,0:T(8,128)(2,1)S(1)} async-done(((bf16[8,128,512]{2,1,0:T(8,128)(2,1)}), bf16[8,128,512]{2,1,0:T(8,128)(2,1)S(1)}, u32[]{:S(2)}, u32[]{:S(2)}) %all-to-all-start.3) | async-done | bytes 1048608 | tf_op jit(solution)/shard_map/all_to_all | solution.py:57
  154.0 1.7 bitcast_convert_fusion.1
  155.7 15.1 %convolution_convert_fusion = bf16[1024,7424]{1,0:T(8,128)(2,1)} fusion(bf16[512,3696]{0,1:T(8,128)(2,1)} %param.27, bf16[512,3696]{0,1:T(8,128)(2,1)} %param.26, f32[1024,512]{1,0:T(8,128)} %bitcast_convert_fusion.1, f32[512]{0:T(512)S(1)} %convert_element_type.160), kind=kOutput, calls=%fused_computation.4 | convolution fusion | flops 7823687680 | bytes 24872960 | tf_op jit(solution)/shard_map/dot_general | solution.py:160
  171.2 34.4 %psum.7 = f32[1024]{0:T(1024)S(1)} all-reduce(f32[1024]{0:T(1024)S(1)} %bitcast.112), channel_id=1, replica_groups=mesh['req'=16,'kv'=8] {'req'}, use_global_device_ids=true, to_apply=%region_10.11 | all-reduce | flops 1024 | bytes 8192 | tf_op jit(solution)/shard_map/psum | solution.py:148
  205.7 96.7 %reduce-scatter.2.cloned.1.call-done = bf16[64,7424]{1,0:T(8,128)(2,1)} async-done(((bf16[1024,7424]{1,0:T(8,128)(2,1)}), bf16[64,7424]{1,0:T(8,128)(2,1)}) %reduce-scatter.2.cloned.1.call-update) | async-done | bytes 950288 | tf_op jit(solution)/shard_map/reduce_scatter | solution.py:159
  302.3 2.3 multiply_convert_fusion.4
  304.7 67.5 %all-gather.2.cloned.1.call-done = bf16[1024,3696]{1,0:T(8,128)(2,1)} async-done(((bf16[64,3696]{1,0:T(8,128)(2,1)}), bf16[1024,3696]{1,0:T(8,128)(2,1)}) %all-gather.2.cloned.1.call-update) | async-done | bytes 7569424 | tf_op jit(solution)/shard_map/all_gather | solution.py:170
  372.2 8.4 %convolution_convert_fusion.2 = bf16[1024,512]{1,0:T(8,128)(2,1)S(1)} fusion(bf16[1024,3696]{1,0:T(8,128)(2,1)} %all-gather.2.cloned.1.call-done, bf16[3696,512]{1,0:T(8,128)(2,1)} %param.28), kind=kOutput, calls=%fused_computation.30 | convolution fusion | flops 3876061184 | bytes 12402688 | tf_op jit(solution)/shard_map/dot_general | solution.py:169
  380.6 20.2 %all_to_all.31 = bf16[8,128,512]{2,1,0:T(8,128)(2,1)S(1)} all-to-all(bf16[8,128,512]{2,1,0:T(8,128)(2,1)S(1)} %bitcast.103), channel_id=1, replica_groups=mesh['req'=16,'kv'=8] {'kv'}, dimensions={0} | all-to-all | bytes 2097152 | tf_op jit(solution)/shard_map/all_to_all | solution.py:51
  402.2 18.3 %all_to_all.32 = bf16[8,128,512]{2,1,0:T(8,128)(2,1)S(1)} all-to-all(bf16[8,128,512]{2,1,0:T(8,128)(2,1)S(1)} %broadcast_in_dim.76), channel_id=1, replica_groups=mesh['req'=16,'kv'=8] {'kv'}, dimensions={0} | all-to-all | bytes 2097152 | tf_op jit(solution)/shard_map/all_to_all | solution.py:57
  (76 shorter events, 13.6 us)
Async XLA Ops:
  6.5 57.5 %copy-start = (bf16[1,8192,1,128]{3,1,2,0:T(8,128)(2,1)S(1)}, bf16[1,8192,1,128]{3,1,2,0:T(8,128)(2,1)}, u32[]{:S(2)}) copy-start(bf16[1,8192,1,128]{3,1,2,0:T(8,128)(2,1)} %param.32) | copy-start | bytes 6291460
  14.1 8.2 %copy-start.8 = (s32[64]{0:T(128)S(1)}, s32[64]{0:T(128)}, u32[]{:S(2)}) copy-start(s32[64]{0:T(128)} %param.35) | copy-start | bytes 772
  14.1 8.2 %copy-start.9 = (s32[16]{0:T(128)S(1)}, s32[16]{0:T(128)}, u32[]{:S(2)}) copy-start(s32[16]{0:T(128)} %param.34) | copy-start | bytes 196
  14.1 9.5 %copy-start.4 = (bf16[1280]{0:T(1024)(128)(2,1)S(1)}, bf16[1280]{0:T(1024)(128)(2,1)}, u32[]{:S(2)}) copy-start(bf16[1280]{0:T(1024)(128)(2,1)} %param.23) | copy-start | bytes 7684
  14.1 9.5 %copy-start.6 = (s32[64]{0:T(128)S(1)}, s32[64]{0:T(128)}, u32[]{:S(2)}) copy-start(s32[64]{0:T(128)} %param.31) | copy-start | bytes 772
  14.1 45.9 %all-to-all-start = ((bf16[16,64,1408]{2,1,0:T(8,128)(2,1)}), bf16[16,64,1408]{2,1,0:T(8,128)(2,1)}, u32[]{:S(2)}, u32[]{:S(2)}) async-start(bf16[16,64,1408]{2,1,0:T(8,128)(2,1)} %bitcast.95), calls=%async_computation | async-start | bytes 5767168 | tf_op jit(solution)/shard_map/all_to_all | solution.py:93
  63.4 2.2 copy-start.3
  73.0 37.3 %copy-start.7 = (bf16[1024,512]{1,0:T(8,128)(2,1)S(1)}, bf16[1024,512]{1,0:T(8,128)(2,1)}, u32[]{:S(2)}) copy-start(bf16[1024,512]{1,0:T(8,128)(2,1)} %param.24) | copy-start | bytes 3145732
  110.3 7.0 %copy-start.2 = (bf16[1024,512]{1,0:T(8,128)(2,1)S(1)}, bf16[1024,512]{1,0:T(8,128)(2,1)}, u32[]{:S(2)}) copy-start(bf16[1024,512]{1,0:T(8,128)(2,1)} %param.20) | copy-start | bytes 3145732
  112.5 19.9 %all-to-all-start.2 = ((bf16[8,128,512]{2,1,0:T(8,128)(2,1)}), bf16[8,128,512]{2,1,0:T(8,128)(2,1)S(1)}, u32[]{:S(2)}, u32[]{:S(2)}) async-start(bf16[8,128,512]{2,1,0:T(8,128)(2,1)} %bitcast.30), calls=%async_computation.2 | async-start | bytes 2097152 | tf_op jit(solution)/shard_map/all_to_all | solution.py:51
  119.0 19.5 %copy-start.5 = (bf16[512]{0:T(512)(128)(2,1)S(1)}, bf16[512]{0:T(512)(128)(2,1)}, u32[]{:S(2)}) copy-start(bf16[512]{0:T(512)(128)(2,1)} %param.25) | copy-start | bytes 3076
  134.7 19.4 %all-to-all-start.3 = ((bf16[8,128,512]{2,1,0:T(8,128)(2,1)}), bf16[8,128,512]{2,1,0:T(8,128)(2,1)S(1)}, u32[]{:S(2)}, u32[]{:S(2)}) async-start(bf16[8,128,512]{2,1,0:T(8,128)(2,1)} %broadcast_in_dim.45), calls=%async_computation.3 | async-start | bytes 2097152 | tf_op jit(solution)/shard_map/all_to_all | solution.py:57
  138.2 164.1 %reduce-scatter.2.cloned.1.call-start = ((), (), s32[]{:S(2)}) async-start(), calls=%async_computation.7 | async-start | bytes 16154624 | tf_op jit(solution)/shard_map/reduce_scatter | solution.py:159
  170.8 201.4 %all-gather.2.cloned.1.call-start = ((), (), s32[]{:S(2)}) async-start(), calls=%async_computation.8 | async-start | bytes 8077312 | tf_op jit(solution)/shard_map/all_gather | solution.py:170
  400.9 20.6 %copy-start.1 = (bf16[1,8192,1,128]{3,1,2,0:T(8,128)(2,1)S(1)}, bf16[1,8192,1,128]{3,1,2,0:T(8,128)(2,1)}, u32[]{:S(2)}) copy-start(bf16[1,8192,1,128]{3,1,2,0:T(8,128)(2,1)} %param.32) | copy-start | bytes 6291460
Sparse Core Ops, SparseCore 0:
  170.9 131.3 reduce-scatter.1
  304.8 67.3 all-gather.1

commit v5 on v3

--- a/solution.py
+++ b/solution.py
@@ -82,17 +82,13 @@
     kv_slot = lax.axis_index("kv")
     n_req = tokens.shape[0] // REQ_DEV
     n_kv = lax.psum(1, "kv")
-    square_part = jnp.sum(wide * wide, axis=1)
-    square_hi = square_part.astype(jnp.bfloat16)
-    square_lo = (square_part - square_hi.astype(jnp.float32)).astype(jnp.bfloat16)
-    square_cols = jnp.pad(jnp.stack([square_hi, square_lo], axis=1), ((0, 0), (0, 126)))
+    square_in = lax.psum(jnp.sum(wide * wide, axis=1), "req")
     gained = (wide * norm_in.astype(jnp.float32)[None, :]).astype(jnp.bfloat16)
     qkv_part = jnp.dot(gained, w_qkv, preferred_element_type=jnp.float32).astype(jnp.bfloat16)
     width = qkv_part.shape[1]
-    sent = jnp.concatenate([qkv_part, square_cols], axis=1).reshape(n_req, REQ_DEV, width + 128)
-    got = lax.all_to_all(sent, "req", 0, 0, tiled=False).astype(jnp.float32)
-    united = jnp.sum(got[:, :, :width], axis=0)
-    square_in = jnp.sum(got[:, :, width] + got[:, :, width + 1], axis=0)
+    got = lax.all_to_all(qkv_part.reshape(n_req, REQ_DEV, width), "req", 0, 0, tiled=False)
+    united = jnp.sum(got.astype(jnp.float32), axis=0)
+    square_in = lax.dynamic_slice_in_dim(square_in, slot * REQ_DEV, REQ_DEV)
     scale_in = lax.rsqrt(square_in / D + EPS)
     united = (united * scale_in[:, None] + qkv_bias.astype(jnp.float32)[None, :]).reshape(
         REQ_DEV, heads_here, GROUP + 2, HD

time: 429 us -> 446 us (1.040)
  blocking collectives: 110 us -> 165 us
  waiting for transfers between devices: 229 us -> 193 us
    psum x0 -> x1, blocking collectives: none -> 60.2 us  [per_device(): square_in = lax.psum(jnp.sum(wide * wide, axis=1), 'req')]
    all_to_all x1, waiting for transfers between devices: 36.1 us -> 0.01 us  [per_device(): lax.all_to_all(qkv_part.reshape(n_req, REQ_DEV, width), 'req', 0, 0, tile...]
    all_to_all x1, blocking collectives: 36.9 us -> 32 us  [per_device(): lax.all_to_all(jnp.broadcast_to(attended[None], (n_req,) + attended.shape...]
  transfers between devices with their start and end apart: 5 -> 5, of which waited for: 5 -> 4; matrix products, arithmetic and copies ran while one was open for 1% -> 1% of each run, Pallas kernels for 0% -> 0%
where the time goes in v5:
time: 446 us; the launch traced here: 445 us
  waiting for transfers between devices  193 us (43%)
  blocking collectives  165 us (37%)
  matrix products  36.4 us (8%)
  starting transfers between devices  16.8 us (4%)
  other arithmetic  15.8 us (4%)
  between operations  13.8 us (3%)
    reduce_scatter x1, waiting for transfers between devices, per_device(): lax.psum_scatter(jnp.dot(mixed_in, w_gate_up, preferred_element_type=jnp....  96.5 us
    all_gather x1, waiting for transfers between devices, per_device(): lax.all_gather(act, 'req', axis=0, tiled=True)  67.5 us
    psum x1, blocking collectives, per_device(): square_in = lax.psum(jnp.sum(wide * wide, axis=1), 'req')  60.2 us
    psum x1, blocking collectives, per_device(): square_mid = lax.psum(jnp.sum(resid_wide * resid_wide, axis=1), 'req')  34.5 us
    all_to_all x1, blocking collectives, per_device(): lax.all_to_all(jnp.broadcast_to(attended[None], (n_req,) + attended.shape...  32 us
    all_to_all x1, blocking collectives, kv_sum(): lax.all_to_all(part.astype(jnp.bfloat16).reshape(n_kv, rows, part.shape[1...  20.2 us
    all_to_all x1, blocking collectives, kv_sum(): return lax.all_to_all(spread, 'kv', 0, 0, tiled=False).reshape(part.shape)  18.3 us
    all_to_all x1, waiting for transfers between devices, kv_sum(): return lax.all_to_all(spread, 'kv', 0, 0, tiled=False).reshape(part.shape)  15.6 us
  transfers between devices with their start and end apart: 5, of which 4 were waited for; matrix products, arithmetic and copies ran while one was open for 1% of the time, Pallas kernels for 0%

profile of v5, /device:TPU:0, one launch (start us, length us, event | category | flops | bytes accessed | tf_op | source)
XLA Modules:
  0.0 445.3 jit_solution(9267483916281028315)
XLA Ops:
  7.4 4.7 %convolution_convert_fusion.1 = bf16[1024,1280]{1,0:T(8,128)(2,1)} fusion(bf16[512,1280]{1,0:T(8,128)(2,1)} %param.22, f32[512]{0:T(512)S(1)} %convert_element_type.100, bf16[1024,512]{1,0:T(8,128)(2,1)} %param.20), kind=kOutput, calls=%fused_computation.17 | convolution fusion | flops 1345060864 | bytes 4982784 | tf_op jit(solution)/shard_map/dot_general | solution.py:87
  12.1 8.2 %all-to-all-start = ((bf16[16,64,1280]{2,1,0:T(8,128)(2,1)}), bf16[16,64,1280]{2,1,0:T(8,128)(2,1)}, u32[]{:S(2)}, u32[]{:S(2)}) async-start(bf16[16,64,1280]{2,1,0:T(8,128)(2,1)} %bitcast.95), calls=%async_computation | async-start | bytes 5242880 | tf_op jit(solution)/shard_map/all_to_all | solution.py:89
  21.2 60.2 %psum.14 = f32[1024]{0:T(1024)S(1)} all-reduce(f32[1024]{0:T(1024)S(1)} %multiply_reduce_fusion.1), channel_id=1, replica_groups=mesh['req'=16,'kv'=8] {'req'}, use_global_device_ids=true, to_apply=%region_2.0 | all-reduce | flops 1024 | bytes 8192 | tf_op jit(solution)/shard_map/psum | solution.py:85
  83.6 2.1 convert_reduce_fusion
  86.6 1.3 multiply_add_fusion
  90.3 1.3 fusion.76
  92.6 3.0 fusion.23
  96.6 32.0 %all_to_all.30 = bf16[16,64,1024]{2,1,0:T(8,128)(2,1)S(1)} all-to-all(bf16[16,64,1024]{2,1,0:T(8,128)(2,1)S(1)} %broadcast_in_dim.44), channel_id=1, replica_groups=mesh['req'=16,'kv'=8] {'req'}, dimensions={0} | all-to-all | bytes 4194304 | tf_op jit(solution)/shard_map/all_to_all | solution.py:136
  128.5 2.2 convolution_convert_fusion.3
  130.7 4.8 %all-to-all-start.2 = ((bf16[8,128,512]{2,1,0:T(8,128)(2,1)}), bf16[8,128,512]{2,1,0:T(8,128)(2,1)S(1)}, u32[]{:S(2)}, u32[]{:S(2)}) async-start(bf16[8,128,512]{2,1,0:T(8,128)(2,1)} %bitcast.102), calls=%async_computation.2 | async-start | bytes 2097152 | tf_op jit(solution)/shard_map/all_to_all | solution.py:51
  135.5 1.6 convert_element_type.99
  137.1 13.5 %all-to-all-done.2 = bf16[8,128,512]{2,1,0:T(8,128)(2,1)S(1)} async-done(((bf16[8,128,512]{2,1,0:T(8,128)(2,1)}), bf16[8,128,512]{2,1,0:T(8,128)(2,1)S(1)}, u32[]{:S(2)}, u32[]{:S(2)}) %all-to-all-start.2) | async-done | bytes 1048608 | tf_op jit(solution)/shard_map/all_to_all | solution.py:51
  152.8 3.6 all-to-all-start.3
  156.6 15.6 %all-to-all-done.3 = bf16[8,128,512]{2,1,0:T(8,128)(2,1)S(1)} async-done(((bf16[8,128,512]{2,1,0:T(8,128)(2,1)}), bf16[8,128,512]{2,1,0:T(8,128)(2,1)S(1)}, u32[]{:S(2)}, u32[]{:S(2)}) %all-to-all-start.3) | async-done | bytes 1048608 | tf_op jit(solution)/shard_map/all_to_all | solution.py:57
  172.5 15.2 %convolution_convert_fusion = bf16[1024,7424]{1,0:T(8,128)(2,1)} fusion(bf16[512,3696]{0,1:T(8,128)(2,1)} %param.27, bf16[512,3696]{0,1:T(8,128)(2,1)} %param.26, f32[1024,512]{1,0:T(8,128)S(1)} %bitcast_convert_fusion.1, f32[512]{0:T(512)S(1)} %convert_element_type.114), kind=kOutput, calls=%fused_computation.4 | convolution fusion | flops 7823687680 | bytes 24872960 | tf_op jit(solution)/shard_map/dot_general | solution.py:156
  188.1 34.5 %psum.15 = f32[1024]{0:T(1024)S(1)} all-reduce(f32[1024]{0:T(1024)S(1)} %bitcast.110), channel_id=1, replica_groups=mesh['req'=16,'kv'=8] {'req'}, use_global_device_ids=true, to_apply=%region_10.11 | all-reduce | flops 1024 | bytes 8192 | tf_op jit(solution)/shard_map/psum | solution.py:144
  222.7 96.5 %reduce-scatter.2.cloned.1.call-done = bf16[64,7424]{1,0:T(8,128)(2,1)} async-done(((bf16[1024,7424]{1,0:T(8,128)(2,1)}), bf16[64,7424]{1,0:T(8,128)(2,1)}) %reduce-scatter.2.cloned.1.call-update) | async-done | bytes 950288 | tf_op jit(solution)/shard_map/reduce_scatter | solution.py:155
  319.2 1.3 convert_element_type.117
  320.5 1.1 fusion.39
  321.6 67.5 %all-gather.2.cloned.1.call-done = bf16[1024,3696]{1,0:T(8,128)(2,1)} async-done(((bf16[64,3696]{1,0:T(8,128)(2,1)}), bf16[1024,3696]{1,0:T(8,128)(2,1)}) %all-gather.2.cloned.1.call-update) | async-done | bytes 7569424 | tf_op jit(solution)/shard_map/all_gather | solution.py:166
  389.1 8.4 %convolution_convert_fusion.2 = bf16[1024,512]{1,0:T(8,128)(2,1)S(1)} fusion(bf16[1024,3696]{1,0:T(8,128)(2,1)} %all-gather.2.cloned.1.call-done, bf16[3696,512]{1,0:T(8,128)(2,1)} %param.28), kind=kOutput, calls=%fused_computation.27 | convolution fusion | flops 3876061184 | bytes 12402688 | tf_op jit(solution)/shard_map/dot_general | solution.py:165
  397.6 20.2 %all_to_all.31 = bf16[8,128,512]{2,1,0:T(8,128)(2,1)S(1)} all-to-all(bf16[8,128,512]{2,1,0:T(8,128)(2,1)S(1)} %bitcast.103), channel_id=1, replica_groups=mesh['req'=16,'kv'=8] {'kv'}, dimensions={0} | all-to-all | bytes 2097152 | tf_op jit(solution)/shard_map/all_to_all | solution.py:51
  418.0 1.1 add_convert_fusion
  419.2 18.3 %all_to_all.32 = bf16[8,128,512]{2,1,0:T(8,128)(2,1)S(1)} all-to-all(bf16[8,128,512]{2,1,0:T(8,128)(2,1)S(1)} %broadcast_in_dim.76), channel_id=1, replica_groups=mesh['req'=16,'kv'=8] {'kv'}, dimensions={0} | all-to-all | bytes 2097152 | tf_op jit(solution)/shard_map/all_to_all | solution.py:57
  (82 shorter events, 13.2 us)
Async XLA Ops:
  6.5 82.6 %copy-start = (bf16[1,8192,1,128]{3,1,2,0:T(8,128)(2,1)S(1)}, bf16[1,8192,1,128]{3,1,2,0:T(8,128)(2,1)}, u32[]{:S(2)}) copy-start(bf16[1,8192,1,128]{3,1,2,0:T(8,128)(2,1)} %param.32) | copy-start | bytes 6291460
  12.1 8.2 %copy-start.13 = (s32[64]{0:T(128)S(1)}, s32[64]{0:T(128)}, u32[]{:S(2)}) copy-start(s32[64]{0:T(128)} %param.35) | copy-start | bytes 772
  12.1 8.3 %copy-start.14 = (s32[16]{0:T(128)S(1)}, s32[16]{0:T(128)}, u32[]{:S(2)}) copy-start(s32[16]{0:T(128)} %param.34) | copy-start | bytes 196
  12.1 8.9 %copy-start.2 = (bf16[1024,512]{1,0:T(8,128)(2,1)S(1)}, bf16[1024,512]{1,0:T(8,128)(2,1)}, u32[]{:S(2)}) copy-start(bf16[1024,512]{1,0:T(8,128)(2,1)} %param.20) | copy-start | bytes 3145732
  12.1 70.6 %copy-start.7 = (bf16[1280]{0:T(1024)(128)(2,1)S(1)}, bf16[1280]{0:T(1024)(128)(2,1)}, u32[]{:S(2)}) copy-start(bf16[1280]{0:T(1024)(128)(2,1)} %param.23) | copy-start | bytes 7684
  12.1 70.6 %copy-start.11 = (s32[64]{0:T(128)S(1)}, s32[64]{0:T(128)}, u32[]{:S(2)}) copy-start(s32[64]{0:T(128)} %param.31) | copy-start | bytes 772
  12.1 71.5 %all-to-all-start = ((bf16[16,64,1280]{2,1,0:T(8,128)(2,1)}), bf16[16,64,1280]{2,1,0:T(8,128)(2,1)}, u32[]{:S(2)}, u32[]{:S(2)}) async-start(bf16[16,64,1280]{2,1,0:T(8,128)(2,1)} %bitcast.95), calls=%async_computation | async-start | bytes 5242880 | tf_op jit(solution)/shard_map/all_to_all | solution.py:89
  20.3 63.3 %copy-start.8 = (f32[64]{0:T(128)}, f32[64]{0:T(128)S(1)}, u32[]{:S(2)}) copy-start(f32[64]{0:T(128)S(1)} %convert_element_type.104) | copy-start | bytes 772
  81.4 2.2 copy-start.9
  86.6 3.7 copy-start.3
  86.6 3.7 copy-start.6
  92.6 3.1 copy-start.5
  96.5 32.0 %copy-start.12 = (bf16[1024,512]{1,0:T(8,128)(2,1)S(1)}, bf16[1024,512]{1,0:T(8,128)(2,1)}, u32[]{:S(2)}) copy-start(bf16[1024,512]{1,0:T(8,128)(2,1)} %param.24) | copy-start | bytes 3145732
  130.7 19.9 %all-to-all-start.2 = ((bf16[8,128,512]{2,1,0:T(8,128)(2,1)}), bf16[8,128,512]{2,1,0:T(8,128)(2,1)S(1)}, u32[]{:S(2)}, u32[]{:S(2)}) async-start(bf16[8,128,512]{2,1,0:T(8,128)(2,1)} %bitcast.102), calls=%async_computation.2 | async-start | bytes 2097152 | tf_op jit(solution)/shard_map/all_to_all | solution.py:51
  137.1 19.5 %copy-start.10 = (bf16[512]{0:T(512)(128)(2,1)S(1)}, bf16[512]{0:T(512)(128)(2,1)}, u32[]{:S(2)}) copy-start(bf16[512]{0:T(512)(128)(2,1)} %param.25) | copy-start | bytes 3076
  152.8 19.4 %all-to-all-start.3 = ((bf16[8,128,512]{2,1,0:T(8,128)(2,1)}), bf16[8,128,512]{2,1,0:T(8,128)(2,1)S(1)}, u32[]{:S(2)}, u32[]{:S(2)}) async-start(bf16[8,128,512]{2,1,0:T(8,128)(2,1)} %broadcast_in_dim.45), calls=%async_computation.3 | async-start | bytes 2097152 | tf_op jit(solution)/shard_map/all_to_all | solution.py:57
  156.4 162.8 %reduce-scatter.2.cloned.1.call-start = ((), (), s32[]{:S(2)}) async-start(), calls=%async_computation.7 | async-start | bytes 16154624 | tf_op jit(solution)/shard_map/reduce_scatter | solution.py:155
  172.5 15.2 %copy-start.4 = (f32[1024,512]{1,0:T(8,128)}, f32[1024,512]{1,0:T(8,128)S(1)}, u32[]{:S(2)}) copy-start(f32[1024,512]{1,0:T(8,128)S(1)} %bitcast_convert_fusion.1) | copy-start | bytes 6291460
  187.8 201.4 %all-gather.2.cloned.1.call-start = ((), (), s32[]{:S(2)}) async-start(), calls=%async_computation.8 | async-start | bytes 8077312 | tf_op jit(solution)/shard_map/all_gather | solution.py:166
  418.0 20.5 %copy-start.1 = (bf16[1,8192,1,128]{3,1,2,0:T(8,128)(2,1)S(1)}, bf16[1,8192,1,128]{3,1,2,0:T(8,128)(2,1)}, u32[]{:S(2)}) copy-start(bf16[1,8192,1,128]{3,1,2,0:T(8,128)(2,1)} %param.32) | copy-start | bytes 6291460
Sparse Core Ops, SparseCore 0:
  187.9 131.2 reduce-scatter.1
  321.7 67.3 all-gather.1

commit v6 on v3

--- a/solution.py
+++ b/solution.py
@@ -149,12 +149,14 @@
     mixed_in = (resid_wide * norm_mid.astype(jnp.float32)[None, :]).astype(jnp.bfloat16)
     units = w_gate.shape[1]
     padded = -(-units // 128) * 128
-    w_gate_up = jnp.concatenate(
-        [
-            jnp.pad(w_gate, ((0, 0), (0, padded - units))),
-            jnp.pad(w_up, ((0, 0), (0, padded - units))),
-        ],
-        axis=1,
+    w_gate_up = lax.optimization_barrier(
+        jnp.concatenate(
+            [
+                jnp.pad(w_gate, ((0, 0), (0, padded - units))),
+                jnp.pad(w_up, ((0, 0), (0, padded - units))),
+            ],
+            axis=1,
+        )
     )
     gate_up = lax.psum_scatter(
         jnp.dot(mixed_in, w_gate_up, preferred_element_type=jnp.float32).astype(jnp.bfloat16),

time: 429 us -> 429 us (level)
  other arithmetic: 17.9 us -> 24.4 us
  waiting for transfers between devices: 229 us -> 223 us
    concatenate x0 -> x1, other arithmetic: none -> 6.6 us  [per_device(): jnp.concatenate([jnp.pad(w_gate, ((0, 0), (0, padded - units))), jnp.pad(...]
    all_to_all x1, waiting for transfers between devices: 15.6 us -> 8.97 us  [kv_sum(): return lax.all_to_all(spread, 'kv', 0, 0, tiled=False).reshape(part.shape)]
  transfers between devices with their start and end apart: 5 -> 5, of which waited for: 5 -> 5; matrix products, arithmetic and copies ran while one was open for 1% -> 2% of each run, Pallas kernels for 0% -> 0%
where the time goes in v6:
time: 429 us; the launch traced here: 428 us
  waiting for transfers between devices  223 us (52%)
  blocking collectives  110 us (26%)
  matrix products  36 us (8%)
  other arithmetic  24.4 us (6%)
  starting transfers between devices  16.9 us (4%)
  between operations  13.8 us (3%)
    reduce_scatter x1, waiting for transfers between devices, per_device(): lax.psum_scatter(jnp.dot(mixed_in, w_gate_up, preferred_element_type=jnp....  96.7 us
    all_gather x1, waiting for transfers between devices, per_device(): lax.all_gather(act, 'req', axis=0, tiled=True)  67.6 us
    all_to_all x1, blocking collectives, per_device(): lax.all_to_all(jnp.broadcast_to(attended[None], (n_req,) + attended.shape...  36.9 us
    all_to_all x1, waiting for transfers between devices, per_device(): got = lax.all_to_all(sent, 'req', 0, 0, tiled=False).astype(jnp.float32)  36.1 us
    psum x1, blocking collectives, per_device(): square_mid = lax.psum(jnp.sum(resid_wide * resid_wide, axis=1), 'req')  34.4 us
    all_to_all x1, blocking collectives, kv_sum(): lax.all_to_all(part.astype(jnp.bfloat16).reshape(n_kv, rows, part.shape[1...  20.4 us
    all_to_all x1, blocking collectives, kv_sum(): return lax.all_to_all(spread, 'kv', 0, 0, tiled=False).reshape(part.shape)  18.3 us
    dot_general x1, matrix products, per_device(): jnp.dot(mixed_in, w_gate_up, preferred_element_type=jnp.float32)  14.9 us
  transfers between devices with their start and end apart: 5, of which 5 were waited for; matrix products, arithmetic and copies ran while one was open for 2% of the time, Pallas kernels for 0%

profile of v6, /device:TPU:0, one launch (start us, length us, event | category | flops | bytes accessed | tf_op | source)
XLA Modules:
  0.0 428.0 jit_solution(12403566622969060213)
XLA Ops:
  6.5 1.6 multiply_reduce_fusion.1
  9.1 3.2 convolution_convert_fusion.1
  12.3 1.8 fusion.9
  14.1 8.2 %all-to-all-start = ((bf16[16,64,1408]{2,1,0:T(8,128)(2,1)}), bf16[16,64,1408]{2,1,0:T(8,128)(2,1)}, u32[]{:S(2)}, u32[]{:S(2)}) async-start(bf16[16,64,1408]{2,1,0:T(8,128)(2,1)} %bitcast.96), calls=%async_computation | async-start | bytes 5767168 | tf_op jit(solution)/shard_map/all_to_all | solution.py:93
  24.0 36.1 %all-to-all-done = bf16[16,64,1408]{2,1,0:T(8,128)(2,1)} async-done(((bf16[16,64,1408]{2,1,0:T(8,128)(2,1)}), bf16[16,64,1408]{2,1,0:T(8,128)(2,1)}, u32[]{:S(2)}, u32[]{:S(2)}) %all-to-all-start) | async-done | bytes 2883616 | tf_op jit(solution)/shard_map/all_to_all | solution.py:93
  60.1 2.4 convert_element_type.142
  67.6 2.9 fusion.19
  70.5 2.0 fusion.28
  73.0 36.9 %all_to_all.30 = bf16[16,64,1024]{2,1,0:T(8,128)(2,1)S(1)} all-to-all(bf16[16,64,1024]{2,1,0:T(8,128)(2,1)S(1)} %broadcast_in_dim.44), channel_id=1, replica_groups=mesh['req'=16,'kv'=8] {'req'}, dimensions={0} | all-to-all | bytes 4194304 | tf_op jit(solution)/shard_map/all_to_all | solution.py:140
  109.9 2.2 convolution_convert_fusion.3
  112.1 4.9 %all-to-all-start.2 = ((bf16[8,128,512]{2,1,0:T(8,128)(2,1)}), bf16[8,128,512]{2,1,0:T(8,128)(2,1)S(1)}, u32[]{:S(2)}, u32[]{:S(2)}) async-start(bf16[8,128,512]{2,1,0:T(8,128)(2,1)} %bitcast.30), calls=%async_computation.2 | async-start | bytes 2097152 | tf_op jit(solution)/shard_map/all_to_all | solution.py:51
  117.0 1.6 convert_element_type.135
  118.7 13.5 %all-to-all-done.2 = bf16[8,128,512]{2,1,0:T(8,128)(2,1)S(1)} async-done(((bf16[8,128,512]{2,1,0:T(8,128)(2,1)}), bf16[8,128,512]{2,1,0:T(8,128)(2,1)S(1)}, u32[]{:S(2)}, u32[]{:S(2)}) %all-to-all-start.2) | async-done | bytes 1048608 | tf_op jit(solution)/shard_map/all_to_all | solution.py:51
  134.4 3.6 all-to-all-start.3
  138.2 6.6 %fusion.3 = bf16[512,7424]{0,1:T(8,128)(2,1)} fusion(bf16[512,3696]{0,1:T(8,128)(2,1)} %param.27, bf16[512,3696]{0,1:T(8,128)(2,1)} %param.26), kind=kLoop, calls=%fused_computation.7 | loop fusion | flops 30408704 | bytes 15171584 | tf_op jit(solution)/shard_map/concatenate | solution.py:153
  144.8 9.0 %all-to-all-done.3 = bf16[8,128,512]{2,1,0:T(8,128)(2,1)S(1)} async-done(((bf16[8,128,512]{2,1,0:T(8,128)(2,1)}), bf16[8,128,512]{2,1,0:T(8,128)(2,1)S(1)}, u32[]{:S(2)}, u32[]{:S(2)}) %all-to-all-start.3) | async-done | bytes 1048608 | tf_op jit(solution)/shard_map/all_to_all | solution.py:57
  153.7 1.7 bitcast_convert_fusion.1
  155.4 14.9 %convolution_convert_fusion = bf16[1024,7424]{1,0:T(8,128)(2,1)} fusion(bf16[512,7424]{0,1:T(8,128)(2,1)} %fusion.3, f32[1024,512]{1,0:T(8,128)} %bitcast_convert_fusion.1, f32[512]{0:T(512)S(1)} %convert_element_type.153), kind=kOutput, calls=%fused_computation.4 | convolution fusion | flops 7793278976 | bytes 24905728 | tf_op jit(solution)/shard_map/dot_general | solution.py:162
  170.7 34.4 %psum.7 = f32[1024]{0:T(1024)S(1)} all-reduce(f32[1024]{0:T(1024)S(1)} %bitcast.113), channel_id=1, replica_groups=mesh['req'=16,'kv'=8] {'req'}, use_global_device_ids=true, to_apply=%region_10.11 | all-reduce | flops 1024 | bytes 8192 | tf_op jit(solution)/shard_map/psum | solution.py:148
  205.2 96.7 %reduce-scatter.2.cloned.1.call-done = bf16[64,7424]{1,0:T(8,128)(2,1)} async-done(((bf16[1024,7424]{1,0:T(8,128)(2,1)}), bf16[64,7424]{1,0:T(8,128)(2,1)}) %reduce-scatter.2.cloned.1.call-update) | async-done | bytes 950288 | tf_op jit(solution)/shard_map/reduce_scatter | solution.py:161
  304.3 67.6 %all-gather.2.cloned.1.call-done = bf16[1024,3696]{1,0:T(8,128)(2,1)} async-done(((bf16[64,3696]{1,0:T(8,128)(2,1)}), bf16[1024,3696]{1,0:T(8,128)(2,1)}) %all-gather.2.cloned.1.call-update) | async-done | bytes 7569424 | tf_op jit(solution)/shard_map/all_gather | solution.py:172
  371.9 8.4 %convolution_convert_fusion.2 = bf16[1024,512]{1,0:T(8,128)(2,1)S(1)} fusion(bf16[1024,3696]{1,0:T(8,128)(2,1)} %all-gather.2.cloned.1.call-done, bf16[3696,512]{1,0:T(8,128)(2,1)} %param.28), kind=kOutput, calls=%fused_computation.26 | convolution fusion | flops 3876061184 | bytes 12402688 | tf_op jit(solution)/shard_map/dot_general | solution.py:171
  380.3 20.4 %all_to_all.31 = bf16[8,128,512]{2,1,0:T(8,128)(2,1)S(1)} all-to-all(bf16[8,128,512]{2,1,0:T(8,128)(2,1)S(1)} %bitcast.104), channel_id=1, replica_groups=mesh['req'=16,'kv'=8] {'kv'}, dimensions={0} | all-to-all | bytes 2097152 | tf_op jit(solution)/shard_map/all_to_all | solution.py:51
  401.9 18.3 %all_to_all.32 = bf16[8,128,512]{2,1,0:T(8,128)(2,1)S(1)} all-to-all(bf16[8,128,512]{2,1,0:T(8,128)(2,1)S(1)} %broadcast_in_dim.76), channel_id=1, replica_groups=mesh['req'=16,'kv'=8] {'kv'}, dimensions={0} | all-to-all | bytes 2097152 | tf_op jit(solution)/shard_map/all_to_all | solution.py:57
  (79 shorter events, 15.3 us)
Async XLA Ops:
  6.5 57.2 %copy-start = (bf16[1,8192,1,128]{3,1,2,0:T(8,128)(2,1)S(1)}, bf16[1,8192,1,128]{3,1,2,0:T(8,128)(2,1)}, u32[]{:S(2)}) copy-start(bf16[1,8192,1,128]{3,1,2,0:T(8,128)(2,1)} %param.32) | copy-start | bytes 6291460
  14.1 8.2 %copy-start.8 = (s32[64]{0:T(128)S(1)}, s32[64]{0:T(128)}, u32[]{:S(2)}) copy-start(s32[64]{0:T(128)} %param.35) | copy-start | bytes 772
  14.1 8.2 %copy-start.9 = (s32[16]{0:T(128)S(1)}, s32[16]{0:T(128)}, u32[]{:S(2)}) copy-start(s32[16]{0:T(128)} %param.34) | copy-start | bytes 196
  14.1 9.5 %copy-start.4 = (bf16[1280]{0:T(1024)(128)(2,1)S(1)}, bf16[1280]{0:T(1024)(128)(2,1)}, u32[]{:S(2)}) copy-start(bf16[1280]{0:T(1024)(128)(2,1)} %param.23) | copy-start | bytes 7684
  14.1 9.5 %copy-start.6 = (s32[64]{0:T(128)S(1)}, s32[64]{0:T(128)}, u32[]{:S(2)}) copy-start(s32[64]{0:T(128)} %param.31) | copy-start | bytes 772
  14.1 45.9 %all-to-all-start = ((bf16[16,64,1408]{2,1,0:T(8,128)(2,1)}), bf16[16,64,1408]{2,1,0:T(8,128)(2,1)}, u32[]{:S(2)}, u32[]{:S(2)}) async-start(bf16[16,64,1408]{2,1,0:T(8,128)(2,1)} %bitcast.96), calls=%async_computation | async-start | bytes 5767168 | tf_op jit(solution)/shard_map/all_to_all | solution.py:93
  63.1 2.2 copy-start.3
  72.5 37.4 %copy-start.7 = (bf16[1024,512]{1,0:T(8,128)(2,1)S(1)}, bf16[1024,512]{1,0:T(8,128)(2,1)}, u32[]{:S(2)}) copy-start(bf16[1024,512]{1,0:T(8,128)(2,1)} %param.24) | copy-start | bytes 3145732
  109.9 7.1 %copy-start.2 = (bf16[1024,512]{1,0:T(8,128)(2,1)S(1)}, bf16[1024,512]{1,0:T(8,128)(2,1)}, u32[]{:S(2)}) copy-start(bf16[1024,512]{1,0:T(8,128)(2,1)} %param.20) | copy-start | bytes 3145732
  112.1 6.5 %copy-start.5 = (bf16[512]{0:T(512)(128)(2,1)S(1)}, bf16[512]{0:T(512)(128)(2,1)}, u32[]{:S(2)}) copy-start(bf16[512]{0:T(512)(128)(2,1)} %param.25) | copy-start | bytes 3076
  112.1 20.0 %all-to-all-start.2 = ((bf16[8,128,512]{2,1,0:T(8,128)(2,1)}), bf16[8,128,512]{2,1,0:T(8,128)(2,1)S(1)}, u32[]{:S(2)}, u32[]{:S(2)}) async-start(bf16[8,128,512]{2,1,0:T(8,128)(2,1)} %bitcast.30), calls=%async_computation.2 | async-start | bytes 2097152 | tf_op jit(solution)/shard_map/all_to_all | solution.py:51
  134.4 19.4 %all-to-all-start.3 = ((bf16[8,128,512]{2,1,0:T(8,128)(2,1)}), bf16[8,128,512]{2,1,0:T(8,128)(2,1)S(1)}, u32[]{:S(2)}, u32[]{:S(2)}) async-start(bf16[8,128,512]{2,1,0:T(8,128)(2,1)} %broadcast_in_dim.45), calls=%async_computation.3 | async-start | bytes 2097152 | tf_op jit(solution)/shard_map/all_to_all | solution.py:57
  137.9 163.9 %reduce-scatter.2.cloned.1.call-start = ((), (), s32[]{:S(2)}) async-start(), calls=%async_computation.7 | async-start | bytes 16154624 | tf_op jit(solution)/shard_map/reduce_scatter | solution.py:161
  170.4 201.5 %all-gather.2.cloned.1.call-start = ((), (), s32[]{:S(2)}) async-start(), calls=%async_computation.8 | async-start | bytes 8077312 | tf_op jit(solution)/shard_map/all_gather | solution.py:172
  380.3 40.9 %copy-start.1 = (bf16[1,8192,1,128]{3,1,2,0:T(8,128)(2,1)S(1)}, bf16[1,8192,1,128]{3,1,2,0:T(8,128)(2,1)}, u32[]{:S(2)}) copy-start(bf16[1,8192,1,128]{3,1,2,0:T(8,128)(2,1)} %param.32) | copy-start | bytes 6291460
Sparse Core Ops, SparseCore 0:
  170.5 131.3 reduce-scatter.1
  304.4 67.4 all-gather.1

commit v7 on v6

--- a/solution.py
+++ b/solution.py
@@ -168,8 +168,11 @@
     gate = gate_up[:, :units] * scale_mid[:, None]
     up = gate_up[:, padded : padded + units] * scale_mid[:, None]
     act = (jax.nn.silu(gate) * up).astype(jnp.bfloat16)
+    act = jnp.pad(act, ((0, 0), (0, padded - units)))
     down_part = jnp.dot(
-        lax.all_gather(act, "req", axis=0, tiled=True), w_down, preferred_element_type=jnp.float32
+        lax.all_gather(act, "req", axis=0, tiled=True),
+        jnp.pad(w_down, ((0, padded - units), (0, 0))),
+        preferred_element_type=jnp.float32,
     )
     return kv_sum(down_part, resid_wide, kv_slot, n_kv)
 

time: 429 us -> 429 us (level)
  no operation moved by 1% of the time
where the time goes in v7:
time: 429 us; the launch traced here: 428 us
  waiting for transfers between devices  223 us (52%)
  blocking collectives  110 us (26%)
  matrix products  36 us (8%)
  other arithmetic  23.7 us (6%)
  starting transfers between devices  16.9 us (4%)
  between operations  13.8 us (3%)
  local copies, waits for them, and re-layouts  4.83 us (1%)
    reduce_scatter x1, waiting for transfers between devices, per_device(): lax.psum_scatter(jnp.dot(mixed_in, w_gate_up, preferred_element_type=jnp....  96.7 us
    all_gather x1, waiting for transfers between devices, per_device(): lax.all_gather(act, 'req', axis=0, tiled=True)  67.6 us
    all_to_all x1, blocking collectives, per_device(): lax.all_to_all(jnp.broadcast_to(attended[None], (n_req,) + attended.shape...  36.9 us
    all_to_all x1, waiting for transfers between devices, per_device(): got = lax.all_to_all(sent, 'req', 0, 0, tiled=False).astype(jnp.float32)  36.1 us
    psum x1, blocking collectives, per_device(): square_mid = lax.psum(jnp.sum(resid_wide * resid_wide, axis=1), 'req')  34.4 us
    all_to_all x1, blocking collectives, kv_sum(): lax.all_to_all(part.astype(jnp.bfloat16).reshape(n_kv, rows, part.shape[1...  20.4 us
    all_to_all x1, blocking collectives, kv_sum(): return lax.all_to_all(spread, 'kv', 0, 0, tiled=False).reshape(part.shape)  18.3 us
    dot_general x1, matrix products, per_device(): jnp.dot(mixed_in, w_gate_up, preferred_element_type=jnp.float32)  14.9 us
  transfers between devices with their start and end apart: 5, of which 5 were waited for; matrix products, arithmetic and copies ran while one was open for 2% of the time, Pallas kernels for 0%

profile of v7, /device:TPU:0, one launch (start us, length us, event | category | flops | bytes accessed | tf_op | source)
XLA Modules:
  0.0 428.1 jit_solution(12541531963069604290)
XLA Ops:
  6.5 1.6 multiply_reduce_fusion.1
  9.1 3.2 convolution_convert_fusion.1
  12.3 1.8 fusion.11
  14.1 8.2 %all-to-all-start = ((bf16[16,64,1408]{2,1,0:T(8,128)(2,1)}), bf16[16,64,1408]{2,1,0:T(8,128)(2,1)}, u32[]{:S(2)}, u32[]{:S(2)}) async-start(bf16[16,64,1408]{2,1,0:T(8,128)(2,1)} %bitcast.95), calls=%async_computation | async-start | bytes 5767168 | tf_op jit(solution)/shard_map/all_to_all | solution.py:93
  24.0 36.1 %all-to-all-done = bf16[16,64,1408]{2,1,0:T(8,128)(2,1)} async-done(((bf16[16,64,1408]{2,1,0:T(8,128)(2,1)}), bf16[16,64,1408]{2,1,0:T(8,128)(2,1)}, u32[]{:S(2)}, u32[]{:S(2)}) %all-to-all-start) | async-done | bytes 2883616 | tf_op jit(solution)/shard_map/all_to_all | solution.py:93
  60.1 2.4 convert_element_type.146
  67.6 2.9 fusion.24
  70.5 2.0 fusion.33
  73.0 36.9 %all_to_all.30 = bf16[16,64,1024]{2,1,0:T(8,128)(2,1)S(1)} all-to-all(bf16[16,64,1024]{2,1,0:T(8,128)(2,1)S(1)} %broadcast_in_dim.44), channel_id=1, replica_groups=mesh['req'=16,'kv'=8] {'req'}, dimensions={0} | all-to-all | bytes 4194304 | tf_op jit(solution)/shard_map/all_to_all | solution.py:140
  109.9 2.2 convolution_convert_fusion.2
  112.1 4.9 %all-to-all-start.2 = ((bf16[8,128,512]{2,1,0:T(8,128)(2,1)}), bf16[8,128,512]{2,1,0:T(8,128)(2,1)S(1)}, u32[]{:S(2)}, u32[]{:S(2)}) async-start(bf16[8,128,512]{2,1,0:T(8,128)(2,1)} %bitcast.30), calls=%async_computation.2 | async-start | bytes 2097152 | tf_op jit(solution)/shard_map/all_to_all | solution.py:51
  117.0 1.6 convert_element_type.139
  118.7 13.5 %all-to-all-done.2 = bf16[8,128,512]{2,1,0:T(8,128)(2,1)S(1)} async-done(((bf16[8,128,512]{2,1,0:T(8,128)(2,1)}), bf16[8,128,512]{2,1,0:T(8,128)(2,1)S(1)}, u32[]{:S(2)}, u32[]{:S(2)}) %all-to-all-start.2) | async-done | bytes 1048608 | tf_op jit(solution)/shard_map/all_to_all | solution.py:51
  134.4 3.6 all-to-all-start.3
  138.2 6.6 %fusion.3 = bf16[512,7424]{0,1:T(8,128)(2,1)} fusion(bf16[512,3696]{0,1:T(8,128)(2,1)} %param.27, bf16[512,3696]{0,1:T(8,128)(2,1)} %param.26), kind=kLoop, calls=%fused_computation.7 | loop fusion | flops 30408704 | bytes 15171584 | tf_op jit(solution)/shard_map/concatenate | solution.py:153
  144.8 9.0 %all-to-all-done.3 = bf16[8,128,512]{2,1,0:T(8,128)(2,1)S(1)} async-done(((bf16[8,128,512]{2,1,0:T(8,128)(2,1)}), bf16[8,128,512]{2,1,0:T(8,128)(2,1)S(1)}, u32[]{:S(2)}, u32[]{:S(2)}) %all-to-all-start.3) | async-done | bytes 1048608 | tf_op jit(solution)/shard_map/all_to_all | solution.py:57
  153.7 1.7 bitcast_convert_fusion.1
  155.4 14.9 %convolution_convert_fusion = bf16[1024,7424]{1,0:T(8,128)(2,1)} fusion(bf16[512,7424]{0,1:T(8,128)(2,1)} %fusion.3, f32[1024,512]{1,0:T(8,128)} %bitcast_convert_fusion.1, f32[512]{0:T(512)S(1)} %convert_element_type.157), kind=kOutput, calls=%fused_computation.4 | convolution fusion | flops 7793278976 | bytes 24905728 | tf_op jit(solution)/shard_map/dot_general | solution.py:162
  170.7 34.4 %psum.7 = f32[1024]{0:T(1024)S(1)} all-reduce(f32[1024]{0:T(1024)S(1)} %bitcast.112), channel_id=1, replica_groups=mesh['req'=16,'kv'=8] {'req'}, use_global_device_ids=true, to_apply=%region_10.11 | all-reduce | flops 1024 | bytes 8192 | tf_op jit(solution)/shard_map/psum | solution.py:148
  205.2 96.7 %reduce-scatter.2.cloned.1.call-done = bf16[64,7424]{1,0:T(8,128)(2,1)} async-done(((bf16[1024,7424]{1,0:T(8,128)(2,1)}), bf16[64,7424]{1,0:T(8,128)(2,1)}) %reduce-scatter.2.cloned.1.call-update) | async-done | bytes 950288 | tf_op jit(solution)/shard_map/reduce_scatter | solution.py:161
  304.3 67.6 %all-gather.2.cloned.1.call-done = bf16[1024,3712]{1,0:T(8,128)(2,1)} async-done(((bf16[64,3712]{1,0:T(8,128)(2,1)}), bf16[1024,3712]{1,0:T(8,128)(2,1)}) %all-gather.2.cloned.1.call-update) | async-done | bytes 7602192 | tf_op jit(solution)/shard_map/all_gather | solution.py:173
  371.9 8.4 %fusion.15 = bf16[1024,512]{1,0:T(8,128)(2,1)S(1)} fusion(bf16[1024,3712]{1,0:T(8,128)(2,1)} %all-gather.2.cloned.1.call-done, bf16[3696,512]{1,0:T(8,128)(2,1)} %param.28), kind=kOutput, calls=%fused_computation.28 | convolution fusion | flops 3892838400 | bytes 12435456 | tf_op jit(solution)/shard_map/dot_general | solution.py:172
  380.4 20.4 %all_to_all.31 = bf16[8,128,512]{2,1,0:T(8,128)(2,1)S(1)} all-to-all(bf16[8,128,512]{2,1,0:T(8,128)(2,1)S(1)} %bitcast.103), channel_id=1, replica_groups=mesh['req'=16,'kv'=8] {'kv'}, dimensions={0} | all-to-all | bytes 2097152 | tf_op jit(solution)/shard_map/all_to_all | solution.py:51
  402.0 18.3 %all_to_all.32 = bf16[8,128,512]{2,1,0:T(8,128)(2,1)S(1)} all-to-all(bf16[8,128,512]{2,1,0:T(8,128)(2,1)S(1)} %broadcast_in_dim.76), channel_id=1, replica_groups=mesh['req'=16,'kv'=8] {'kv'}, dimensions={0} | all-to-all | bytes 2097152 | tf_op jit(solution)/shard_map/all_to_all | solution.py:57
  (80 shorter events, 15.4 us)
Async XLA Ops:
  6.5 57.2 %copy-start = (bf16[1,8192,1,128]{3,1,2,0:T(8,128)(2,1)S(1)}, bf16[1,8192,1,128]{3,1,2,0:T(8,128)(2,1)}, u32[]{:S(2)}) copy-start(bf16[1,8192,1,128]{3,1,2,0:T(8,128)(2,1)} %param.32) | copy-start | bytes 6291460
  14.1 8.2 %copy-start.8 = (s32[64]{0:T(128)S(1)}, s32[64]{0:T(128)}, u32[]{:S(2)}) copy-start(s32[64]{0:T(128)} %param.35) | copy-start | bytes 772
  14.1 8.2 %copy-start.9 = (s32[16]{0:T(128)S(1)}, s32[16]{0:T(128)}, u32[]{:S(2)}) copy-start(s32[16]{0:T(128)} %param.34) | copy-start | bytes 196
  14.1 9.5 %copy-start.4 = (bf16[1280]{0:T(1024)(128)(2,1)S(1)}, bf16[1280]{0:T(1024)(128)(2,1)}, u32[]{:S(2)}) copy-start(bf16[1280]{0:T(1024)(128)(2,1)} %param.23) | copy-start | bytes 7684
  14.1 9.5 %copy-start.6 = (s32[64]{0:T(128)S(1)}, s32[64]{0:T(128)}, u32[]{:S(2)}) copy-start(s32[64]{0:T(128)} %param.31) | copy-start | bytes 772
  14.1 45.9 %all-to-all-start = ((bf16[16,64,1408]{2,1,0:T(8,128)(2,1)}), bf16[16,64,1408]{2,1,0:T(8,128)(2,1)}, u32[]{:S(2)}, u32[]{:S(2)}) async-start(bf16[16,64,1408]{2,1,0:T(8,128)(2,1)} %bitcast.95), calls=%async_computation | async-start | bytes 5767168 | tf_op jit(solution)/shard_map/all_to_all | solution.py:93
  63.1 2.2 copy-start.3
  72.5 37.4 %copy-start.7 = (bf16[1024,512]{1,0:T(8,128)(2,1)S(1)}, bf16[1024,512]{1,0:T(8,128)(2,1)}, u32[]{:S(2)}) copy-start(bf16[1024,512]{1,0:T(8,128)(2,1)} %param.24) | copy-start | bytes 3145732
  109.9 7.1 %copy-start.2 = (bf16[1024,512]{1,0:T(8,128)(2,1)S(1)}, bf16[1024,512]{1,0:T(8,128)(2,1)}, u32[]{:S(2)}) copy-start(bf16[1024,512]{1,0:T(8,128)(2,1)} %param.20) | copy-start | bytes 3145732
  112.1 6.5 %copy-start.5 = (bf16[512]{0:T(512)(128)(2,1)S(1)}, bf16[512]{0:T(512)(128)(2,1)}, u32[]{:S(2)}) copy-start(bf16[512]{0:T(512)(128)(2,1)} %param.25) | copy-start | bytes 3076
  112.1 20.0 %all-to-all-start.2 = ((bf16[8,128,512]{2,1,0:T(8,128)(2,1)}), bf16[8,128,512]{2,1,0:T(8,128)(2,1)S(1)}, u32[]{:S(2)}, u32[]{:S(2)}) async-start(bf16[8,128,512]{2,1,0:T(8,128)(2,1)} %bitcast.30), calls=%async_computation.2 | async-start | bytes 2097152 | tf_op jit(solution)/shard_map/all_to_all | solution.py:51
  134.4 19.4 %all-to-all-start.3 = ((bf16[8,128,512]{2,1,0:T(8,128)(2,1)}), bf16[8,128,512]{2,1,0:T(8,128)(2,1)S(1)}, u32[]{:S(2)}, u32[]{:S(2)}) async-start(bf16[8,128,512]{2,1,0:T(8,128)(2,1)} %broadcast_in_dim.45), calls=%async_computation.3 | async-start | bytes 2097152 | tf_op jit(solution)/shard_map/all_to_all | solution.py:57
  137.9 163.9 %reduce-scatter.2.cloned.1.call-start = ((), (), s32[]{:S(2)}) async-start(), calls=%async_computation.7 | async-start | bytes 16154624 | tf_op jit(solution)/shard_map/reduce_scatter | solution.py:161
  170.4 201.6 %all-gather.2.cloned.1.call-start = ((), (), s32[]{:S(2)}) async-start(), calls=%async_computation.8 | async-start | bytes 8077312 | tf_op jit(solution)/shard_map/all_gather | solution.py:173
  380.4 40.9 %copy-start.1 = (bf16[1,8192,1,128]{3,1,2,0:T(8,128)(2,1)S(1)}, bf16[1,8192,1,128]{3,1,2,0:T(8,128)(2,1)}, u32[]{:S(2)}) copy-start(bf16[1,8192,1,128]{3,1,2,0:T(8,128)(2,1)} %param.32) | copy-start | bytes 6291460
Sparse Core Ops, SparseCore 0:
  170.5 131.3 reduce-scatter.1
  304.5 67.4 all-gather.1
